TPU v7x, 256 devices: a whole 4x4x8 slice. The times are simulated.
256 devices in a mesh: expert: 32 (over z_lo, x, core), replica: 8 (over z_hi, y).
Axes of the slice: x: 4, y: 4, z: 8 (z_hi: 2, z_lo: 4; z = z_hi * 4 + z_lo), core: 2. Of those that a mesh axis runs over, the one named last changes fastest.
Arguments:
- tokens: bfloat16 [2048, 4096], P(('expert', 'replica')), may hold values from -6 to 6
- expert_ids: int32 [2048, 8], P(('expert', 'replica')), may hold values from 0 to 31, as said below
- gate_weights: float32 [2048, 8], P(('expert', 'replica')), may hold values from 0.1 to 1
- expert_holder: int32 [32], replicated, may hold values from 0 to 31, each once
- swap_pairs: int32 [8, 2], replicated, may hold values from 0 to 31, as said below
- capacity: int32 [32], replicated, may hold values from 2 to 4, as said below
- w_gate: bfloat16 [32, 1536, 4096], P('expert', 'replica'), may hold values from -0.09375 to 0.09375
- w_up: bfloat16 [32, 1536, 4096], P('expert', 'replica'), may hold values from -0.09375 to 0.09375
- w_down: bfloat16 [32, 1536, 4096], P('expert', 'replica'), may hold values from -0.15625 to 0.15625
Outputs:
- moe_output: bfloat16 [2048, 4096], P(('expert', 'replica'))
- moved_gate: bfloat16 [32, 1536, 4096], P('expert', 'replica')
- moved_up: bfloat16 [32, 1536, 4096], P('expert', 'replica')
- moved_down: bfloat16 [32, 1536, 4096], P('expert', 'replica')
- expert_peak: float32 [32], P('expert')
Inputs may be any that keep to these rules, and one draw needn't show every extreme that they name: `expert_ids`: each token names 8 different experts; among one device's 8 tokens no expert is named more than 4 times, and one expert is named exactly 4 times by the tokens of every device. `swap_pairs`: no index appears twice; the two indices of every pair differ by 16. The expert named 4 times by every device has capacity 4. `expert_holder`: each index of the expert axis holds one expert.
All inputs are finite; a program needn't handle non-finite values.
Results may differ from a plain program's by a relative error of at most 0.014.
Values may be sent and summed in bfloat16 or wider, within the bound.
No kernel may reach another device: no remote copies, remote signals or barrier semaphores. Data moves between devices by JAX's collectives and lax.ppermute only.
A program may use at most 128 MiB of HBM per device.

v0:
```python
import jax
import jax.numpy as jnp
from jax import lax
from jax.sharding import PartitionSpec as P

TOPK = 8
CAP = 4


def pair_partner(swap_pairs, device_count):
    devices = jnp.arange(device_count, dtype=jnp.int32)
    first_dev = swap_pairs[:, 0:1]
    second_dev = swap_pairs[:, 1:2]
    offsets = jnp.where(devices[None, :] == first_dev, second_dev - first_dev, 0)
    offsets = offsets + jnp.where(devices[None, :] == second_dev, first_dev - second_dev, 0)
    return devices + jnp.sum(offsets, axis=0)


def table_lookup(values_table, positions):
    matches = positions[..., None] == jnp.arange(values_table.shape[0], dtype=jnp.int32)
    return jnp.sum(jnp.where(matches, values_table, 0), axis=-1)


def route_slots(expert_ids, holder_now, capacity):
    expert_count = holder_now.shape[0]
    flat_ids = expert_ids.reshape(-1)
    chosen = (flat_ids[:, None] == jnp.arange(expert_count, dtype=jnp.int32)[None, :]).astype(
        jnp.int32
    )
    earlier = jnp.cumsum(chosen, axis=0) - chosen
    ranking = jnp.sum(earlier * chosen, axis=1)
    slot_kept = ranking < table_lookup(capacity, flat_ids)
    target = table_lookup(holder_now, flat_ids)
    slot_ids = jnp.where(slot_kept, target * CAP + ranking, -1)
    matched = slot_ids[None, :] == jnp.arange(expert_count * CAP, dtype=jnp.int32)[:, None]
    owners = jnp.arange(flat_ids.shape[0], dtype=jnp.int32) // TOPK
    source = jnp.sum(jnp.where(matched, owners[None, :], 0), axis=1)
    filled = jnp.any(matched, axis=1)
    return (jnp.maximum(slot_ids, 0), slot_kept, source, filled)


def expert_hidden(row_block, gate_local, up_local):
    leading = row_block.shape[:-1]
    row_matrix = row_block.reshape(-1, row_block.shape[-1])
    contract = (((1,), (1,)), ((), ()))
    gate_value = lax.dot_general(
        row_matrix, gate_local, contract, preferred_element_type=jnp.float32
    )
    up_value = lax.dot_general(row_matrix, up_local, contract, preferred_element_type=jnp.float32)
    hidden = (jax.nn.silu(gate_value) * up_value).astype(jnp.bfloat16)
    return hidden.reshape(leading + (gate_local.shape[0],))


def shards(
    tokens, expert_ids, gate_weights, expert_holder, swap_pairs, capacity, w_gate, w_up, w_down
):
    experts = lax.axis_size("expert")
    replicas = lax.axis_size("replica")
    tok_rows, width = tokens.shape
    partner = pair_partner(swap_pairs, experts)
    holder_after = table_lookup(partner, expert_holder)
    spread = (
        lax.all_to_all(
            w_gate.reshape(experts, -1), "expert", split_axis=0, concat_axis=0, tiled=True
        ),
        lax.all_to_all(
            w_up.reshape(experts, -1), "expert", split_axis=0, concat_axis=0, tiled=True
        ),
        lax.all_to_all(
            w_down.reshape(experts, -1), "expert", split_axis=0, concat_axis=0, tiled=True
        ),
    )
    arranged = tuple((jnp.take(pieces, partner, axis=0) for pieces in spread))
    moved = (
        lax.all_to_all(arranged[0], "expert", split_axis=0, concat_axis=0, tiled=True),
        lax.all_to_all(arranged[1], "expert", split_axis=0, concat_axis=0, tiled=True),
        lax.all_to_all(arranged[2], "expert", split_axis=0, concat_axis=0, tiled=True),
    )
    moved_gate = moved[0].reshape(w_gate.shape)
    moved_up = moved[1].reshape(w_up.shape)
    moved_down = moved[2].reshape(w_down.shape)
    gate_local, up_local, down_local = (moved_gate[0], moved_up[0], moved_down[0])
    group_tokens, group_ids = (
        lax.all_gather(tokens, "replica", axis=0, tiled=True),
        lax.all_gather(expert_ids, "replica", axis=0, tiled=True),
    )
    group_ids = group_ids.reshape(replicas, tok_rows, TOPK)
    slot_all, kept_all, source_all, filled_all = jax.vmap(route_slots, in_axes=(0, None, None))(
        group_ids, holder_after, capacity
    )
    starts = jnp.arange(replicas, dtype=jnp.int32)[:, None] * tok_rows
    picked = jnp.take(group_tokens, source_all + starts, axis=0)
    outgoing = jnp.where(filled_all[:, :, None], picked, jnp.zeros((), jnp.bfloat16))
    hidden = expert_hidden(
        lax.all_to_all(
            outgoing.reshape(replicas, experts, CAP, width),
            "expert",
            split_axis=1,
            concat_axis=1,
            tiled=True,
        ),
        gate_local,
        up_local,
    )
    replica_index = lax.axis_index("replica")
    slot_of = lax.dynamic_index_in_dim(slot_all, replica_index, 0, keepdims=False)
    slot_kept = lax.dynamic_index_in_dim(kept_all, replica_index, 0, keepdims=False)
    hidden_rows = hidden.reshape(-1, hidden.shape[-1])
    local_peak = jnp.max(jnp.abs(hidden_rows)).astype(jnp.float32)
    summed = lax.psum_scatter(
        jnp.dot(hidden_rows, down_local, preferred_element_type=jnp.float32).astype(jnp.bfloat16),
        "replica",
        scatter_dimension=0,
        tiled=True,
    )
    results = summed.reshape(experts, CAP, width)
    returned = lax.all_to_all(results, "expert", split_axis=0, concat_axis=0, tiled=True)
    fetched = jnp.take(returned.reshape(experts * CAP, width), slot_of, axis=0).reshape(
        tok_rows, TOPK, width
    )
    scales = jnp.where(slot_kept, gate_weights.reshape(-1), jnp.float32(0.0)).reshape(
        tok_rows, TOPK, 1
    )
    moe_output = jnp.sum(scales * fetched, axis=1).astype(jnp.bfloat16)
    expert_peak = lax.pmax(local_peak, "replica")
    return (moe_output, moved_gate, moved_up, moved_down, expert_peak.reshape(1))


def solution(mesh):
    placed = (
        P(("expert", "replica"), None),
        P(("expert", "replica"), None),
        P(("expert", "replica"), None),
        P(),
        P(),
        P(),
        P("expert", "replica", None),
        P("expert", "replica", None),
        P("expert", "replica", None),
    )
    return jax.shard_map(
        shards,
        mesh=mesh,
        in_specs=placed,
        out_specs=(
            P(("expert", "replica"), None),
            P("expert", "replica", None),
            P("expert", "replica", None),
            P("expert", "replica", None),
            P("expert"),
        ),
        check_vma=False,
    )
```

profile of v0, /device:TPU:2, one launch (start us, length us, event | category | flops | bytes accessed | tf_op | source)
XLA Modules:
  0.0 886.4 jit_solution(17751766660079716728)
XLA Ops:
  13.0 11.4 %reduce.13 = bf16[32,24576]{1,0:T(8,128)(2,1)} reduce(bf16[32,1,24576]{2,1,0:T(2,128)(2,1)S(1)} %all_to_all.65, bf16[]{:T(256)} %broadcast.166), dimensions={1}, to_apply=%all_to_all.65.reduce_sub_computation | reduce | bytes 3145730 | tf_op jit(solution)/shard_map/all_to_all | solution.py:63
  27.6 9.5 %all-to-all-start.1 = ((bf16[32,2,12288]{2,1,0:T(2,128)(2,1)}), bf16[32,2,12288]{2,1,0:T(2,128)(2,1)}, u32[]{:S(2)}, u32[]{:S(2)}) async-start(bf16[32,2,12288]{2,1,0:T(2,128)(2,1)} %reshape.259), calls=%async_computation.1 | async-start | bytes 3145728 | tf_op jit(solution)/shard_map/all_to_all | solution.py:63
  42.5 11.4 %reduce.12 = bf16[32,24576]{1,0:T(8,128)(2,1)} reduce(bf16[32,1,24576]{2,1,0:T(2,128)(2,1)S(1)} %all_to_all.66, bf16[]{:T(256)} %broadcast.166), dimensions={1}, to_apply=%all_to_all.66.reduce_sub_computation | reduce | bytes 3145730 | tf_op jit(solution)/shard_map/all_to_all | solution.py:66
  57.1 17.1 %all-to-all-done.1 = bf16[32,2,12288]{2,1,0:T(2,128)(2,1)} async-done(((bf16[32,2,12288]{2,1,0:T(2,128)(2,1)}), bf16[32,2,12288]{2,1,0:T(2,128)(2,1)}, u32[]{:S(2)}, u32[]{:S(2)}) %all-to-all-start.1) | async-done | bytes 1572896 | tf_op jit(solution)/shard_map/all_to_all | solution.py:63
  86.1 11.4 %reduce.11 = bf16[32,24576]{1,0:T(8,128)(2,1)} reduce(bf16[32,1,24576]{2,1,0:T(2,128)(2,1)S(1)} %all_to_all.67, bf16[]{:T(256)} %broadcast.166), dimensions={1}, to_apply=%all_to_all.67.reduce_sub_computation | reduce | bytes 3145730 | tf_op jit(solution)/shard_map/all_to_all | solution.py:69
  100.7 17.1 %all-to-all-done.3 = bf16[32,2,12288]{2,1,0:T(2,128)(2,1)} async-done(((bf16[32,2,12288]{2,1,0:T(2,128)(2,1)}), bf16[32,2,12288]{2,1,0:T(2,128)(2,1)}, u32[]{:S(2)}, u32[]{:S(2)}) %all-to-all-start.3) | async-done | bytes 1572896 | tf_op jit(solution)/shard_map/all_to_all | solution.py:66
  124.2 9.5 %reshape.260 = bf16[32,1,24576]{2,1,0:T(2,128)(2,1)} reshape(bf16[32,2,12288]{2,1,0:T(2,128)(2,1)} %all-to-all-done.1) | data formatting | bytes 3145728
  137.3 9.5 %reshape.256 = bf16[32,1,24576]{2,1,0:T(2,128)(2,1)} reshape(bf16[32,2,12288]{2,1,0:T(2,128)(2,1)} %all-to-all-done.3) | data formatting | bytes 3145728
  161.1 9.5 %reshape.264 = bf16[32,1,24576]{2,1,0:T(2,128)(2,1)} reshape(bf16[32,2,12288]{2,1,0:T(2,128)(2,1)} %all-to-all-done.5) | data formatting | bytes 3145728
  199.8 31.5 %all-to-all-done.2 = bf16[32,2,12288]{2,1,0:T(2,128)(2,1)} async-done(((bf16[32,2,12288]{2,1,0:T(2,128)(2,1)}), bf16[32,2,12288]{2,1,0:T(2,128)(2,1)}, u32[]{:S(2)}, u32[]{:S(2)}) %all-to-all-start.2) | async-done | bytes 1572896 | tf_op jit(solution)/shard_map/all_to_all | solution.py:75
  237.2 67.2 %all_gather.6 = s32[64,8]{1,0:T(8,128)S(1)} all-gather(s32[8,8]{1,0:T(8,128)S(1)} %copy-done.5), channel_id=1, replica_groups=mesh['expert'=32,'replica'=8] {'replica'}, dimensions={0}, use_global_device_ids=true | all-gather | bytes 2304 | tf_op jit(solution)/shard_map/all_gather | solution.py:85
  322.6 60.6 %all_gather.7 = bf16[64,4096]{1,0:T(8,128)(2,1)S(1)} all-gather(bf16[8,4096]{1,0:T(8,128)(2,1)S(1)} %copy-done.4), channel_id=1, replica_groups=mesh['expert'=32,'replica'=8] {'replica'}, dimensions={0}, use_global_device_ids=true | all-gather | bytes 589824 | tf_op jit(solution)/shard_map/all_gather | solution.py:84
  391.0 13.1 %gather.16 = bf16[8,32,4,4096]{3,2,1,0:T(4,128)(2,1)} reshape(bf16[1024,4096]{1,0:T(8,128)(2,1)} %gather_fusion) | data formatting | bytes 16777216 | tf_op jit(solution)/shard_map/jit(_take)/gather | solution.py:92
  405.0 8.6 fusion
  422.0 9.9 %reshape.262 = bf16[32,1,24576]{2,1,0:T(2,128)(2,1)} reshape(bf16[32,2,12288]{2,1,0:T(2,128)(2,1)} %all-to-all-done.2) | data formatting | bytes 3145728
  431.9 11.2 %reduce.2 = bf16[32,24576]{1,0:T(8,128)(2,1)S(1)} reduce(bf16[32,1,24576]{2,1,0:T(2,128)(2,1)} %reshape.262, bf16[]{:T(256)} %constant.99), dimensions={1}, to_apply=%all_to_all.53.reduce_sub_computation | reduce | bytes 3145730 | tf_op jit(solution)/shard_map/all_to_all | solution.py:75
  449.9 11.2 %reduce.3 = bf16[32,24576]{1,0:T(8,128)(2,1)S(1)} reduce(bf16[32,1,24576]{2,1,0:T(2,128)(2,1)} %reshape.258, bf16[]{:T(256)} %constant.99), dimensions={1}, to_apply=%all_to_all.58.reduce_sub_computation | reduce | bytes 3145730 | tf_op jit(solution)/shard_map/all_to_all | solution.py:76
  463.8 9.7 %reshape.266 = bf16[32,1,24576]{2,1,0:T(2,128)(2,1)} reshape(bf16[32,2,12288]{2,1,0:T(2,128)(2,1)} %all-to-all-done.6) | data formatting | bytes 3145728
  473.5 12.3 %reduce.4 = bf16[32,24576]{1,0:T(8,128)(2,1)} reduce(bf16[32,1,24576]{2,1,0:T(2,128)(2,1)} %reshape.266, bf16[]{:T(256)} %constant.99), dimensions={1}, to_apply=%all_to_all.63.reduce_sub_computation | reduce | bytes 3145730 | tf_op jit(solution)/shard_map/all_to_all | solution.py:77
  489.6 115.8 %all-to-all-done = bf16[8,32,4,4096]{3,2,0,1:T(4,128)(2,1)} async-done(((bf16[8,32,4,4096]{3,2,0,1:T(4,128)(2,1)}), bf16[8,32,4,4096]{3,2,0,1:T(4,128)(2,1)}, u32[]{:S(2)}, u32[]{:S(2)}) %all-to-all-start) | async-done | bytes 8388640 | tf_op jit(solution)/shard_map/all_to_all | solution.py:95
  605.5 8.5 copy.66
  614.0 12.7 %reshape.188 = bf16[1024,4096]{1,0:T(8,128)(2,1)} reshape(bf16[8,32,4,4096]{3,2,1,0:T(4,128)(2,1)} %copy.66) | data formatting | bytes 16777216 | tf_op jit(solution)/shard_map/reshape | solution.py:44
  642.8 184.3 %reduce-scatter.2.cloned.1.call-done = bf16[128,4096]{1,0:T(8,128)(2,1)} async-done(((bf16[1024,4096]{1,0:T(8,128)(2,1)}), bf16[128,4096]{1,0:T(8,128)(2,1)}) %reduce-scatter.2.cloned.1.call-update) | async-done | bytes 1048592 | tf_op jit(solution)/shard_map/reduce_scatter | solution.py:110
  845.1 30.6 %pmax.7 = f32[1]{0:T(128)} all-reduce(bf16[1]{0:T(256)(128)(2,1)} %bitcast.14), channel_id=1, replica_groups=mesh['expert'=32,'replica'=8] {'replica'}, use_global_device_ids=true, to_apply=%region_11.13 | all-reduce | flops 1 | bytes 6 | tf_op jit(solution)/shard_map/pmax | solution.py:125
  (99 shorter events, 177.9 us)
Async XLA Ops:
  27.6 46.5 %all-to-all-start.1 = ((bf16[32,2,12288]{2,1,0:T(2,128)(2,1)}), bf16[32,2,12288]{2,1,0:T(2,128)(2,1)}, u32[]{:S(2)}, u32[]{:S(2)}) async-start(bf16[32,2,12288]{2,1,0:T(2,128)(2,1)} %reshape.259), calls=%async_computation.1 | async-start | bytes 3145728 | tf_op jit(solution)/shard_map/all_to_all | solution.py:63
  74.2 43.6 %all-to-all-start.3 = ((bf16[32,2,12288]{2,1,0:T(2,128)(2,1)}), bf16[32,2,12288]{2,1,0:T(2,128)(2,1)}, u32[]{:S(2)}, u32[]{:S(2)}) async-start(bf16[32,2,12288]{2,1,0:T(2,128)(2,1)} %reshape.255), calls=%async_computation.3 | async-start | bytes 3145728 | tf_op jit(solution)/shard_map/all_to_all | solution.py:66
  100.7 23.4 %copy-start.7 = (s32[8,2]{0,1:T(2,128)S(1)}, s32[8,2]{0,1:T(2,128)}, u32[]{:S(2)}) copy-start(s32[8,2]{0,1:T(2,128)} %param.15) | copy-start | bytes 196
  117.7 43.3 %all-to-all-start.5 = ((bf16[32,2,12288]{2,1,0:T(2,128)(2,1)}), bf16[32,2,12288]{2,1,0:T(2,128)(2,1)}, u32[]{:S(2)}, u32[]{:S(2)}) async-start(bf16[32,2,12288]{2,1,0:T(2,128)(2,1)} %reshape.263), calls=%async_computation.5 | async-start | bytes 3145728 | tf_op jit(solution)/shard_map/all_to_all | solution.py:69
  188.1 43.2 %all-to-all-start.2 = ((bf16[32,2,12288]{2,1,0:T(2,128)(2,1)}), bf16[32,2,12288]{2,1,0:T(2,128)(2,1)}, u32[]{:S(2)}, u32[]{:S(2)}) async-start(bf16[32,2,12288]{2,1,0:T(2,128)(2,1)} %reshape.261), calls=%async_computation.2 | async-start | bytes 3145728 | tf_op jit(solution)/shard_map/all_to_all | solution.py:75
  199.8 37.4 %copy-start.5 = (s32[8,8]{1,0:T(8,128)S(1)}, s32[8,8]{1,0:T(8,128)}, u32[]{:S(2)}) copy-start(s32[8,8]{1,0:T(8,128)} %param.12) | copy-start | bytes 772
  199.8 104.9 %copy-start.9 = (s32[32]{0:T(128)S(1)}, s32[32]{0:T(128)}, u32[]{:S(2)}) copy-start(s32[32]{0:T(128)} %param.14) | copy-start | bytes 388
  231.3 80.6 %all-to-all-start.4 = ((bf16[32,2,12288]{2,1,0:T(2,128)(2,1)}), bf16[32,2,12288]{2,1,0:T(2,128)(2,1)S(1)}, u32[]{:S(2)}, u32[]{:S(2)}) async-start(bf16[32,2,12288]{2,1,0:T(2,128)(2,1)} %reshape.257), calls=%async_computation.4 | async-start | bytes 3145728 | tf_op jit(solution)/shard_map/all_to_all | solution.py:76
  311.9 7.9 copy-start.8
  311.9 10.7 %copy-start.4 = (bf16[8,4096]{1,0:T(8,128)(2,1)S(1)}, bf16[8,4096]{1,0:T(8,128)(2,1)}, u32[]{:S(2)}) copy-start(bf16[8,4096]{1,0:T(8,128)(2,1)} %param.11) | copy-start | bytes 196612
  311.9 101.7 %all-to-all-start.6 = ((bf16[32,2,12288]{2,1,0:T(2,128)(2,1)}), bf16[32,2,12288]{2,1,0:T(2,128)(2,1)}, u32[]{:S(2)}, u32[]{:S(2)}) async-start(bf16[32,2,12288]{2,1,0:T(2,128)(2,1)} %reshape.265), calls=%async_computation.6 | async-start | bytes 3145728 | tf_op jit(solution)/shard_map/all_to_all | solution.py:77
  413.6 191.8 %all-to-all-start = ((bf16[8,32,4,4096]{3,2,0,1:T(4,128)(2,1)}), bf16[8,32,4,4096]{3,2,0,1:T(4,128)(2,1)}, u32[]{:S(2)}, u32[]{:S(2)}) async-start(bf16[8,32,4,4096]{3,2,0,1:T(4,128)(2,1)} %fusion), calls=%async_computation | async-start | bytes 16777216 | tf_op jit(solution)/shard_map/all_to_all | solution.py:95
  421.9 405.2 %reduce-scatter.2.cloned.1.call-start = ((), (), s32[]{:S(2)}) async-start(), calls=%async_computation.9 | async-start | bytes 9437184 | tf_op jit(solution)/shard_map/reduce_scatter | solution.py:110
  626.7 6.9 copy-start.1
  626.7 6.9 copy-start.3
  633.6 3.6 copy-start.2
  829.4 7.6 copy-start.6
  829.4 46.4 %all-to-all-start.7 = ((bf16[32,4,4096]{2,1,0:T(4,128)(2,1)}), bf16[32,4,4096]{2,1,0:T(4,128)(2,1)}, u32[]{:S(2)}, u32[]{:S(2)}) async-start(bf16[32,4,4096]{2,1,0:T(4,128)(2,1)} %reshape.189), calls=%async_computation.8 | async-start | bytes 2097152 | tf_op jit(solution)/shard_map/all_to_all | solution.py:117
  839.7 2.7 copy-start
Sparse Core Ops, SparseCore 0:
  643.0 184.1 reduce-scatter.1
where the time goes:
time: 898 us; the launch traced here: 886 us
  waiting for transfers between devices  371 us (41%)
  local copies, waits for them, and re-layouts  172 us (19%)
  blocking collectives  159 us (18%)
  other arithmetic  96.1 us (11%)
  starting transfers between devices  57.5 us (6%)
  matrix products  16 us (2%)
  between operations  14.8 us (2%)
    reduce_scatter x1, waiting for transfers between devices, shards(): lax.psum_scatter(jnp.dot(hidden_rows, down_local, preferred_element_type=...  184 us
    all_to_all x1, waiting for transfers between devices, shards(): lax.all_to_all(outgoing.reshape(replicas, experts, CAP, width), 'expert',...  116 us
    unnamed x35, local copies, waits for them, and re-layouts  82.2 us
    all_gather x1, blocking collectives, shards(): lax.all_gather(expert_ids, 'replica', axis=0, tiled=True)  67.2 us
    all_gather x1, blocking collectives, shards(): lax.all_gather(tokens, 'replica', axis=0, tiled=True)  60.6 us
    all_to_all x1, waiting for transfers between devices, shards(): lax.all_to_all(arranged[0], 'expert', split_axis=0, concat_axis=0, tiled=...  31.5 us
    pmax x1, blocking collectives, shards(): expert_peak = lax.pmax(local_peak, 'replica')  30.6 us
    gather x2, local copies, waits for them, and re-layouts, shards(): picked = jnp.take(group_tokens, source_all + starts, axis=0)  20.9 us
  transfers between devices with their start and end apart: 9, of which 6 were waited for; matrix products, arithmetic and copies ran while one was open for 21% of the time, Pallas kernels for 0%

commit v1 on v0

--- a/solution.py
+++ b/solution.py
@@ -58,35 +58,22 @@
     replicas = lax.axis_size("replica")
     tok_rows, width = tokens.shape
     partner = pair_partner(swap_pairs, experts)
-    holder_after = table_lookup(partner, expert_holder)
-    spread = (
-        lax.all_to_all(
-            w_gate.reshape(experts, -1), "expert", split_axis=0, concat_axis=0, tiled=True
-        ),
-        lax.all_to_all(
-            w_up.reshape(experts, -1), "expert", split_axis=0, concat_axis=0, tiled=True
-        ),
-        lax.all_to_all(
-            w_down.reshape(experts, -1), "expert", split_axis=0, concat_axis=0, tiled=True
-        ),
+    me = lax.axis_index("expert")
+    swapped = lax.dynamic_index_in_dim(partner, me, 0, keepdims=False) != me
+    half = experts // 2
+    ring = [(d, (d + half) % experts) for d in range(experts)]
+    arrived = tuple(lax.ppermute(w, "expert", ring) for w in (w_gate, w_up, w_down))
+    moved_gate, moved_up, moved_down = (
+        jnp.where(swapped, got, own) for got, own in zip(arrived, (w_gate, w_up, w_down))
     )
-    arranged = tuple((jnp.take(pieces, partner, axis=0) for pieces in spread))
-    moved = (
-        lax.all_to_all(arranged[0], "expert", split_axis=0, concat_axis=0, tiled=True),
-        lax.all_to_all(arranged[1], "expert", split_axis=0, concat_axis=0, tiled=True),
-        lax.all_to_all(arranged[2], "expert", split_axis=0, concat_axis=0, tiled=True),
-    )
-    moved_gate = moved[0].reshape(w_gate.shape)
-    moved_up = moved[1].reshape(w_up.shape)
-    moved_down = moved[2].reshape(w_down.shape)
-    gate_local, up_local, down_local = (moved_gate[0], moved_up[0], moved_down[0])
+    gate_local, up_local, down_local = (w_gate[0], w_up[0], w_down[0])
     group_tokens, group_ids = (
         lax.all_gather(tokens, "replica", axis=0, tiled=True),
         lax.all_gather(expert_ids, "replica", axis=0, tiled=True),
     )
     group_ids = group_ids.reshape(replicas, tok_rows, TOPK)
     slot_all, kept_all, source_all, filled_all = jax.vmap(route_slots, in_axes=(0, None, None))(
-        group_ids, holder_after, capacity
+        group_ids, expert_holder, capacity
     )
     starts = jnp.arange(replicas, dtype=jnp.int32)[:, None] * tok_rows
     picked = jnp.take(group_tokens, source_all + starts, axis=0)
@@ -122,7 +109,8 @@
         tok_rows, TOPK, 1
     )
     moe_output = jnp.sum(scales * fetched, axis=1).astype(jnp.bfloat16)
-    expert_peak = lax.pmax(local_peak, "replica")
+    group_peak = lax.pmax(local_peak, "replica")
+    expert_peak = jnp.where(swapped, lax.ppermute(group_peak, "expert", ring), group_peak)
     return (moe_output, moved_gate, moved_up, moved_down, expert_peak.reshape(1))
 
 

time: 898 us -> 757 us (0.84); the launches traced: 886 us -> 756 us
  blocking collectives: 159 us -> 315 us
  local copies, waits for them, and re-layouts: 172 us -> 44.8 us
  waiting for transfers between devices: 371 us -> 250 us
  other arithmetic: 96.1 us -> 20.3 us
  starting transfers between devices: 57.5 us -> 91.3 us
    ppermute x0 -> x4, waiting for transfers between devices: none -> 250 us  [the longest x3 245 us: shards(): lax.ppermute(w, 'expert', ring)]
    all_to_all x0 -> x1, blocking collectives: none -> 190 us  [shards(): lax.all_to_all(outgoing.reshape(replicas, experts, CAP, width), 'expert',...]
    all_to_all x7 -> x0, waiting for transfers between devices: 187 us -> none  [the longest x1 116 us: shards(): lax.all_to_all(outgoing.reshape(replicas, experts, CAP, width), 'expert',...]
    reduce_scatter x1, waiting for transfers between devices: 184 us -> 0.01 us  [shards(): lax.psum_scatter(jnp.dot(hidden_rows, down_local, preferred_element_type=...]
    unnamed x35 -> x8, local copies, waits for them, and re-layouts: 82.2 us -> 0.02 us
    all_to_all x10 -> x0, other arithmetic: 81.8 us -> none  [the longest x3 18.8 us: shards(): lax.all_to_all(arranged[2], 'expert', split_axis=0, concat_axis=0, tiled=...]
    all_to_all x1, starting transfers between devices: 6.97 us -> 86.8 us  [shards(): lax.all_to_all(results, 'expert', split_axis=0, concat_axis=0, tiled=True)]
    all_to_all x7 -> x0, starting transfers between devices: 50.4 us -> none  [the longest x1 9.49 us: shards(): lax.all_to_all(w_gate.reshape(experts, -1), 'expert', split_axis=0, conca...]
  transfers between devices with their start and end apart: 9 -> 6, of which waited for: 6 -> 2; matrix products, arithmetic and copies ran while one was open for 21% -> 1% of each run, Pallas kernels for 0% -> 0%
where the time goes in v1:
time: 757 us; the launch traced here: 756 us
  blocking collectives  315 us (42%)
  waiting for transfers between devices  250 us (33%)
  starting transfers between devices  91.3 us (12%)
  local copies, waits for them, and re-layouts  44.8 us (6%)
  other arithmetic  20.3 us (3%)
  matrix products  17.6 us (2%)
  between operations  17.3 us (2%)
    ppermute x3, waiting for transfers between devices, shards(): lax.ppermute(w, 'expert', ring)  245 us
    all_to_all x1, blocking collectives, shards(): lax.all_to_all(outgoing.reshape(replicas, experts, CAP, width), 'expert',...  190 us
    all_to_all x1, starting transfers between devices, shards(): lax.all_to_all(results, 'expert', split_axis=0, concat_axis=0, tiled=True)  86.8 us
    all_gather x1, blocking collectives, shards(): lax.all_gather(expert_ids, 'replica', axis=0, tiled=True)  46.4 us
    all_gather x1, blocking collectives, shards(): lax.all_gather(tokens, 'replica', axis=0, tiled=True)  44.8 us
    pmax x1, blocking collectives, shards(): group_peak = lax.pmax(local_peak, 'replica')  34 us
    gather x2, local copies, waits for them, and re-layouts, shards(): picked = jnp.take(group_tokens, source_all + starts, axis=0)  20.8 us
  transfers between devices with their start and end apart: 6, of which 2 were waited for; matrix products, arithmetic and copies ran while one was open for 1% of the time, Pallas kernels for 0%

profile of v1, /device:TPU:2, one launch (start us, length us, event | category | flops | bytes accessed | tf_op | source)
XLA Modules:
  0.0 756.1 jit_solution(8081594906752745250)
XLA Ops:
  7.2 46.4 %all_gather.6 = s32[64,8]{1,0:T(8,128)S(1)} all-gather(s32[8,8]{1,0:T(8,128)} %param.10), channel_id=1, replica_groups=mesh['expert'=32,'replica'=8] {'replica'}, dimensions={0}, use_global_device_ids=true | all-gather | bytes 2304 | tf_op jit(solution)/shard_map/all_gather | solution.py:72
  53.8 1.4 fusion.20
  55.1 3.0 select_reduce_fusion.1
  58.7 44.8 %all_gather.7 = bf16[64,4096]{1,0:T(8,128)(2,1)S(1)} all-gather(bf16[8,4096]{1,0:T(8,128)(2,1)} %param.9), channel_id=1, replica_groups=mesh['expert'=32,'replica'=8] {'replica'}, dimensions={0}, use_global_device_ids=true | all-gather | bytes 589824 | tf_op jit(solution)/shard_map/all_gather | solution.py:71
  103.5 7.7 %gather_fusion = bf16[1024,4096]{1,0:T(8,128)(2,1)} fusion(bf16[64,4096]{1,0:T(8,128)(2,1)S(1)} %all_gather.7, s32[1024]{0:T(1024)S(1)} %fusion.18), kind=kCustom, calls=%fused_computation | custom fusion | bytes 16781312 | tf_op jit(solution)/shard_map/jit(_take)/gather | solution.py:79
  111.3 13.1 %gather.13 = bf16[8,32,4,4096]{3,2,1,0:T(4,128)(2,1)} reshape(bf16[1024,4096]{1,0:T(8,128)(2,1)} %gather_fusion) | data formatting | bytes 16777216 | tf_op jit(solution)/shard_map/jit(_take)/gather | solution.py:79
  125.1 7.3 fusion
  132.4 189.9 %all_to_all.10 = bf16[8,32,4,4096]{3,2,0,1:T(4,128)(2,1)S(1)} all-to-all(bf16[8,32,4,4096]{3,2,0,1:T(4,128)(2,1)S(1)} %fusion), channel_id=1, replica_groups=mesh['expert'=32,'replica'=8] {'expert'}, dimensions={1} | all-to-all | bytes 16777216 | tf_op jit(solution)/shard_map/all_to_all | solution.py:82
  322.3 6.1 copy.51
  328.4 12.5 %reshape.149 = bf16[1024,4096]{1,0:T(8,128)(2,1)} reshape(bf16[8,32,4,4096]{3,2,1,0:T(4,128)(2,1)} %copy.51) | data formatting | bytes 16777216 | tf_op jit(solution)/shard_map/reshape | solution.py:44
  340.9 6.8 fusion.4
  347.8 5.1 abs_reduce_fusion
  352.9 5.6 convolution_convert_fusion
  358.6 1.5 collective-permute-start.2
  360.1 1.5 collective-permute-start.1
  361.6 1.4 collective-permute-start
  365.0 245.1 %collective-permute-done.2 = bf16[1,192,4096]{2,1,0:T(8,128)(2,1)S(1)} collective-permute-done((bf16[1,192,4096]{2,1,0:T(8,128)(2,1)S(1)}, bf16[1,192,4096]{2,1,0:T(8,128)(2,1)S(1)}, u32[]{:S(2)}, u32[]{:S(2)}) %collective-permute-start.2) | collective-permute-done | bytes 1572896 | tf_op jit(solution)/shard_map/ppermute | solution.py:65
  610.1 1.3 broadcast_select_fusion
  611.4 2.3 reshape.150
  613.7 86.8 %all-to-all-start.1 = ((bf16[32,4,4096]{2,1,0:T(4,128)(2,1)}), bf16[32,4,4096]{2,1,0:T(4,128)(2,1)S(1)}, u32[]{:S(2)}, u32[]{:S(2)}) async-start(bf16[32,4,4096]{2,1,0:T(4,128)(2,1)} %reshape.150), calls=%async_computation.2 | async-start | bytes 2097152 | tf_op jit(solution)/shard_map/all_to_all | solution.py:104
  700.5 2.7 broadcast_select_fusion.1
  703.2 2.7 broadcast_select_fusion.2
  706.0 34.0 %pmax.7 = f32[]{:T(128)} all-reduce(bf16[]{:T(256)} %get-tuple-element.13), channel_id=1, replica_groups=mesh['expert'=32,'replica'=8] {'replica'}, use_global_device_ids=true, to_apply=%region_10.11 | all-reduce | flops 1 | bytes 6 | tf_op jit(solution)/shard_map/pmax | solution.py:112
  740.0 4.6 collective-permute-done.3
  (45 shorter events, 5.0 us)
Async XLA Ops:
  7.2 604.3 %reduce-scatter.2.cloned.1.call-start = ((), (), s32[]{:S(2)}) async-start(), calls=%async_computation.3 | async-start | bytes 9437184 | tf_op jit(solution)/shard_map/reduce_scatter | solution.py:97
  340.9 6.8 copy-start
  347.8 5.1 copy-start.1
  358.6 4.5 copy-start.3
  358.6 6.4 copy-start.2
  358.6 251.5 %collective-permute-start.2 = (bf16[1,192,4096]{2,1,0:T(8,128)(2,1)S(1)}, bf16[1,192,4096]{2,1,0:T(8,128)(2,1)S(1)}, u32[]{:S(2)}, u32[]{:S(2)}) collective-permute-start(bf16[1,192,4096]{2,1,0:T(8,128)(2,1)S(1)} %copy-done.1), channel_id=1, source_target_pairs={{0,128},{8,136},{16,144},{24,152},{32,160},{40,168},{48,176},{56,1... | collective-permute-start | bytes 4718600 | tf_op jit(solution)/shard_map/ppermute | solution.py:65
  360.1 340.4 %collective-permute-start.1 = (bf16[1,192,4096]{2,1,0:T(8,128)(2,1)}, bf16[1,192,4096]{2,1,0:T(8,128)(2,1)}, u32[]{:S(2)}, u32[]{:S(2)}) collective-permute-start(bf16[1,192,4096]{2,1,0:T(8,128)(2,1)} %param.16), channel_id=1, source_target_pairs={{0,128},{8,136},{16,144},{24,152},{32,160},{40,168},{48,176},{56,1... | collective-permute-start | bytes 4718600 | tf_op jit(solution)/shard_map/ppermute | solution.py:65
  361.6 341.6 %collective-permute-start = (bf16[1,192,4096]{2,1,0:T(8,128)(2,1)}, bf16[1,192,4096]{2,1,0:T(8,128)(2,1)}, u32[]{:S(2)}, u32[]{:S(2)}) collective-permute-start(bf16[1,192,4096]{2,1,0:T(8,128)(2,1)} %param.15), channel_id=1, source_target_pairs={{0,128},{8,136},{16,144},{24,152},{32,160},{40,168},{48,176},{56,1... | collective-permute-start | bytes 4718600 | tf_op jit(solution)/shard_map/ppermute | solution.py:65
  613.7 132.2 %all-to-all-start.1 = ((bf16[32,4,4096]{2,1,0:T(4,128)(2,1)}), bf16[32,4,4096]{2,1,0:T(4,128)(2,1)S(1)}, u32[]{:S(2)}, u32[]{:S(2)}) async-start(bf16[32,4,4096]{2,1,0:T(4,128)(2,1)} %reshape.150), calls=%async_computation.2 | async-start | bytes 2097152 | tf_op jit(solution)/shard_map/all_to_all | solution.py:104
  740.0 4.6 collective-permute-start.3
Sparse Core Ops, SparseCore 0:
  358.7 222.9 reduce-scatter.1

commit v2 on v1

--- a/solution.py
+++ b/solution.py
@@ -57,51 +57,41 @@
     experts = lax.axis_size("expert")
     replicas = lax.axis_size("replica")
     tok_rows, width = tokens.shape
+    units = w_gate.shape[1]
+    cols = width // replicas
     partner = pair_partner(swap_pairs, experts)
     me = lax.axis_index("expert")
     swapped = lax.dynamic_index_in_dim(partner, me, 0, keepdims=False) != me
     half = experts // 2
     ring = [(d, (d + half) % experts) for d in range(experts)]
     arrived = tuple(lax.ppermute(w, "expert", ring) for w in (w_gate, w_up, w_down))
-    moved_gate, moved_up, moved_down = (
-        jnp.where(swapped, got, own) for got, own in zip(arrived, (w_gate, w_up, w_down))
+    down_cols = lax.all_to_all(
+        w_down[0].reshape(units, replicas, cols),
+        "replica",
+        split_axis=1,
+        concat_axis=0,
+        tiled=True,
+    ).reshape(units * replicas, cols)
+    slot_of, slot_kept, source, filled = route_slots(expert_ids, expert_holder, capacity)
+    outgoing = jnp.where(
+        filled[:, None], jnp.take(tokens, source, axis=0), jnp.zeros((), jnp.bfloat16)
     )
-    gate_local, up_local, down_local = (w_gate[0], w_up[0], w_down[0])
-    group_tokens, group_ids = (
-        lax.all_gather(tokens, "replica", axis=0, tiled=True),
-        lax.all_gather(expert_ids, "replica", axis=0, tiled=True),
-    )
-    group_ids = group_ids.reshape(replicas, tok_rows, TOPK)
-    slot_all, kept_all, source_all, filled_all = jax.vmap(route_slots, in_axes=(0, None, None))(
-        group_ids, expert_holder, capacity
-    )
-    starts = jnp.arange(replicas, dtype=jnp.int32)[:, None] * tok_rows
-    picked = jnp.take(group_tokens, source_all + starts, axis=0)
-    outgoing = jnp.where(filled_all[:, :, None], picked, jnp.zeros((), jnp.bfloat16))
-    hidden = expert_hidden(
-        lax.all_to_all(
-            outgoing.reshape(replicas, experts, CAP, width),
-            "expert",
-            split_axis=1,
-            concat_axis=1,
-            tiled=True,
-        ),
-        gate_local,
-        up_local,
-    )
-    replica_index = lax.axis_index("replica")
-    slot_of = lax.dynamic_index_in_dim(slot_all, replica_index, 0, keepdims=False)
-    slot_kept = lax.dynamic_index_in_dim(kept_all, replica_index, 0, keepdims=False)
-    hidden_rows = hidden.reshape(-1, hidden.shape[-1])
-    local_peak = jnp.max(jnp.abs(hidden_rows)).astype(jnp.float32)
-    summed = lax.psum_scatter(
-        jnp.dot(hidden_rows, down_local, preferred_element_type=jnp.float32).astype(jnp.bfloat16),
+    arrived_rows = lax.all_to_all(outgoing.reshape(experts, CAP, width), "expert", 0, 0, tiled=True)
+    group_rows = lax.all_gather(arrived_rows, "replica", axis=0, tiled=False)
+    hidden = expert_hidden(group_rows, w_gate[0], w_up[0]).reshape(-1, units)
+    hidden_all = lax.all_gather(hidden, "replica", axis=1, tiled=True)
+    group_peak = jnp.max(jnp.abs(hidden_all)).astype(jnp.float32)
+    out_cols = jnp.dot(
+        hidden_all, down_cols, preferred_element_type=jnp.float32
+    ).astype(jnp.bfloat16)
+    full_rows = lax.all_to_all(
+        out_cols.reshape(replicas, experts, CAP, cols),
         "replica",
-        scatter_dimension=0,
+        split_axis=0,
+        concat_axis=3,
         tiled=True,
     )
-    results = summed.reshape(experts, CAP, width)
-    returned = lax.all_to_all(results, "expert", split_axis=0, concat_axis=0, tiled=True)
+    returned = lax.all_to_all(full_rows.reshape(experts, CAP, width), "expert", 0, 0, tiled=True)
     fetched = jnp.take(returned.reshape(experts * CAP, width), slot_of, axis=0).reshape(
         tok_rows, TOPK, width
     )
@@ -109,7 +99,9 @@
         tok_rows, TOPK, 1
     )
     moe_output = jnp.sum(scales * fetched, axis=1).astype(jnp.bfloat16)
-    group_peak = lax.pmax(local_peak, "replica")
+    moved_gate, moved_up, moved_down = (
+        jnp.where(swapped, got, own) for got, own in zip(arrived, (w_gate, w_up, w_down))
+    )
     expert_peak = jnp.where(swapped, lax.ppermute(group_peak, "expert", ring), group_peak)
     return (moe_output, moved_gate, moved_up, moved_down, expert_peak.reshape(1))
 

time: 757 us -> 585 us (0.77)
  blocking collectives: 315 us -> 34.9 us
  waiting for transfers between devices: 250 us -> 444 us
  starting transfers between devices: 91.3 us -> 29.3 us
  local copies, waits for them, and re-layouts: 44.8 us -> 24.1 us
  other arithmetic: 20.3 us -> 11.3 us
    all_gather x0 -> x2, waiting for transfers between devices: none -> 258 us  [the longest x1 173 us: shards(): group_rows = lax.all_gather(arrived_rows, 'replica', axis=0, tiled=False)]
    all_to_all x1, blocking collectives: 190 us -> 34.9 us  [shards(): lax.all_to_all(outgoing.reshape(experts, CAP, width), 'expert', 0, 0, til...]
    ppermute x3, waiting for transfers between devices: 245 us -> 136 us  [shards(): lax.ppermute(w, 'expert', ring)]
    all_gather x2 -> x0, blocking collectives: 91.2 us -> none  [the longest x1 46.4 us: shards(): lax.all_gather(expert_ids, 'replica', axis=0, tiled=True)]
    all_to_all x1 -> x3, starting transfers between devices: 86.8 us -> 23.9 us  [the longest x1 16.3 us: shards(): lax.all_to_all(full_rows.reshape(experts, CAP, width), 'expert', 0, 0, ti...]
    all_to_all x1 -> x3, waiting for transfers between devices: 0.01 us -> 45.8 us  [the longest x1 45.8 us: shards(): lax.all_to_all(w_down[0].reshape(units, replicas, cols), 'replica', split...]
    pmax x1 -> x0, blocking collectives: 34 us -> none  [shards(): group_peak = lax.pmax(local_peak, 'replica')]
    gather x2, local copies, waits for them, and re-layouts: 20.8 us -> 1.62 us  [shards(): jnp.take(tokens, source, axis=0)]
  transfers between devices with their start and end apart: 6 -> 9, of which waited for: 2 -> 7; matrix products, arithmetic and copies ran while one was open for 1% -> 4% of each run, Pallas kernels for 0% -> 0%
where the time goes in v2:
time: 585 us; the launch traced here: 579 us
  waiting for transfers between devices  444 us (76%)
  blocking collectives  34.9 us (6%)
  starting transfers between devices  29.3 us (5%)
  local copies, waits for them, and re-layouts  24.1 us (4%)
  between operations  18 us (3%)
  matrix products  16.8 us (3%)
  other arithmetic  11.3 us (2%)
    all_gather x1, waiting for transfers between devices, shards(): group_rows = lax.all_gather(arrived_rows, 'replica', axis=0, tiled=False)  173 us
    ppermute x3, waiting for transfers between devices, shards(): lax.ppermute(w, 'expert', ring)  136 us
    all_gather x1, waiting for transfers between devices, shards(): hidden_all = lax.all_gather(hidden, 'replica', axis=1, tiled=True)  84.8 us
    all_to_all x1, waiting for transfers between devices, shards(): lax.all_to_all(w_down[0].reshape(units, replicas, cols), 'replica', split...  45.8 us
    all_to_all x1, blocking collectives, shards(): lax.all_to_all(outgoing.reshape(experts, CAP, width), 'expert', 0, 0, til...  34.9 us
    all_to_all x1, starting transfers between devices, shards(): lax.all_to_all(full_rows.reshape(experts, CAP, width), 'expert', 0, 0, ti...  16.3 us
    reshape x1, local copies, waits for them, and re-layouts, expert_hidden(): row_matrix = row_block.reshape(-1, row_block.shape[-1])  12.5 us
  transfers between devices with their start and end apart: 9, of which 7 were waited for; matrix products, arithmetic and copies ran while one was open for 4% of the time, Pallas kernels for 0%

profile of v2, /device:TPU:2, one launch (start us, length us, event | category | flops | bytes accessed | tf_op | source)
XLA Modules:
  0.0 578.7 jit_solution(9635932873370742258)
XLA Ops:
  11.9 34.9 %all_to_all.40 = bf16[32,4,4096]{2,1,0:T(4,128)(2,1)} all-to-all(bf16[32,4,4096]{2,1,0:T(4,128)(2,1)S(1)} %select_select_fusion), channel_id=1, replica_groups=mesh['expert'=32,'replica'=8] {'expert'}, dimensions={0} | all-to-all | bytes 2097152 | tf_op jit(solution)/shard_map/all_to_all | solution.py:79
  46.9 173.2 %all-gather.6.cloned.1.call-done = bf16[256,4,4096]{2,1,0:T(4,128)(2,1)} async-done(((bf16[32,4,4096]{2,1,0:T(4,128)(2,1)}), bf16[256,4,4096]{2,1,0:T(4,128)(2,1)}) %all-gather.6.cloned.1.call-update) | async-done | bytes 8388624 | tf_op jit(solution)/shard_map/all_gather | solution.py:80
  220.1 12.5 %reshape.150 = bf16[1024,4096]{1,0:T(8,128)(2,1)} reshape(bf16[256,4,4096]{2,1,0:T(4,128)(2,1)} %all-gather.6.cloned.1.call-done) | data formatting | bytes 16777216 | tf_op jit(solution)/shard_map/reshape | solution.py:44
  232.6 6.8 %fusion.2 = f32[1024,192]{0,1:T(8,128)S(1)} fusion(bf16[1024,4096]{1,0:T(8,128)(2,1)} %reshape.150, bf16[1,192,4096]{2,1,0:T(8,128)(2,1)} %param.15), kind=kOutput, calls=%fused_computation.5 | convolution fusion | flops 1610612736 | bytes 10747904 | tf_op jit(solution)/shard_map/dot_general | solution.py:46
  239.5 5.2 fusion.7
  245.4 1.6 copy.23
  247.0 3.7 all-to-all-start.1
  251.7 2.1 collective-permute-start.1
  254.6 45.8 %all-to-all-done.1 = bf16[192,8,512]{2,0,1:T(8,128)(2,1)S(1)} async-done(((bf16[192,8,512]{2,0,1:T(8,128)(2,1)}), bf16[192,8,512]{2,0,1:T(8,128)(2,1)S(1)}, u32[]{:S(2)}, u32[]{:S(2)}) %all-to-all-start.1) | async-done | bytes 1572896 | tf_op jit(solution)/shard_map/all_to_all | solution.py:68
  300.5 84.8 %all-gather.4.cloned.1.call-done = bf16[1024,1536]{0,1:T(8,128)(2,1)} async-done(((bf16[1024,192]{0,1:T(8,128)(2,1)}), bf16[1024,1536]{0,1:T(8,128)(2,1)}) %all-gather.4.cloned.1.call-update) | async-done | bytes 3145744 | tf_op jit(solution)/shard_map/all_gather | solution.py:82
  385.3 4.7 convolution_convert_fusion
  389.9 1.3 reshape.152
  392.5 3.9 all-to-all-start.2
  397.9 79.4 %collective-permute-done.2 = bf16[1,192,4096]{2,1,0:T(8,128)(2,1)} collective-permute-done((bf16[1,192,4096]{2,1,0:T(8,128)(2,1)S(1)}, bf16[1,192,4096]{2,1,0:T(8,128)(2,1)}, u32[]{:S(2)}, u32[]{:S(2)}) %collective-permute-start.2) | collective-permute-done | bytes 1572896 | tf_op jit(solution)/shard_map/ppermute | solution.py:67
  477.4 1.3 broadcast_select_fusion
  479.3 1.6 reshape.175
  480.9 16.3 %all-to-all-start.3 = ((bf16[32,4,4096]{2,1,0:T(4,128)(2,1)}), bf16[32,4,4096]{2,1,0:T(4,128)(2,1)S(1)}, u32[]{:S(2)}, u32[]{:S(2)}) async-start(bf16[32,4,4096]{2,1,0:T(4,128)(2,1)} %reshape.175), calls=%async_computation.3 | async-start | bytes 2097152 | tf_op jit(solution)/shard_map/all_to_all | solution.py:94
  497.2 25.2 %collective-permute-done.1 = bf16[1,192,4096]{2,1,0:T(8,128)(2,1)} collective-permute-done((bf16[1,192,4096]{2,1,0:T(8,128)(2,1)}, bf16[1,192,4096]{2,1,0:T(8,128)(2,1)}, u32[]{:S(2)}, u32[]{:S(2)}) %collective-permute-start.1) | collective-permute-done | bytes 1572896 | tf_op jit(solution)/shard_map/ppermute | solution.py:67
  522.3 2.7 broadcast_select_fusion.1
  525.1 31.0 %collective-permute-done = bf16[1,192,4096]{2,1,0:T(8,128)(2,1)} collective-permute-done((bf16[1,192,4096]{2,1,0:T(8,128)(2,1)}, bf16[1,192,4096]{2,1,0:T(8,128)(2,1)}, u32[]{:S(2)}, u32[]{:S(2)}) %collective-permute-start) | collective-permute-done | bytes 1572896 | tf_op jit(solution)/shard_map/ppermute | solution.py:67
  556.1 2.7 broadcast_select_fusion.2
  558.8 1.3 abs_reduce_fusion
  560.7 1.4 collective-permute-start.3
  562.1 5.0 collective-permute-done.3
  (50 shorter events, 12.1 us)
Async XLA Ops:
  7.2 2.2 copy-start
  7.2 212.9 %all-gather.6.cloned.1.call-start = ((), (), s32[]{:S(2)}) async-start(), calls=%async_computation.5 | async-start | bytes 9437184 | tf_op jit(solution)/shard_map/all_gather | solution.py:80
  46.8 338.4 %all-gather.4.cloned.1.call-start = ((), (), s32[]{:S(2)}) async-start(), calls=%async_computation.4 | async-start | bytes 3538944 | tf_op jit(solution)/shard_map/all_gather | solution.py:82
  232.6 6.9 %copy-start.1 = (bf16[1024,4096]{1,0:T(8,128)(2,1)S(1)}, bf16[1024,4096]{1,0:T(8,128)(2,1)}, u32[]{:S(2)}) copy-start(bf16[1024,4096]{1,0:T(8,128)(2,1)} %reshape.150) | copy-start | bytes 25165828
  239.5 5.3 copy-start.2
  247.0 7.6 %copy-start.5 = (s32[8,2]{0,1:T(2,128)S(1)}, s32[8,2]{0,1:T(2,128)}, u32[]{:S(2)}) copy-start(s32[8,2]{0,1:T(2,128)} %param.13) | copy-start | bytes 196
  247.0 53.4 %all-to-all-start.1 = ((bf16[192,8,512]{2,0,1:T(8,128)(2,1)}), bf16[192,8,512]{2,0,1:T(8,128)(2,1)S(1)}, u32[]{:S(2)}, u32[]{:S(2)}) async-start(bf16[192,8,512]{2,0,1:T(8,128)(2,1)} %copy.23), calls=%async_computation.1 | async-start | bytes 3145728 | tf_op jit(solution)/shard_map/all_to_all | solution.py:68
  250.7 226.6 %collective-permute-start.2 = (bf16[1,192,4096]{2,1,0:T(8,128)(2,1)S(1)}, bf16[1,192,4096]{2,1,0:T(8,128)(2,1)}, u32[]{:S(2)}, u32[]{:S(2)}) collective-permute-start(bf16[1,192,4096]{2,1,0:T(8,128)(2,1)S(1)} %copy-done.2), channel_id=1, source_target_pairs={{0,128},{8,136},{16,144},{24,152},{32,160},{40,168},{48,176},{56,1... | collective-permute-start | bytes 4718600 | tf_op jit(solution)/shard_map/ppermute | solution.py:67
  251.7 270.6 %collective-permute-start.1 = (bf16[1,192,4096]{2,1,0:T(8,128)(2,1)}, bf16[1,192,4096]{2,1,0:T(8,128)(2,1)}, u32[]{:S(2)}, u32[]{:S(2)}) collective-permute-start(bf16[1,192,4096]{2,1,0:T(8,128)(2,1)} %param.16), channel_id=1, source_target_pairs={{0,128},{8,136},{16,144},{24,152},{32,160},{40,168},{48,176},{56,1... | collective-permute-start | bytes 4718600 | tf_op jit(solution)/shard_map/ppermute | solution.py:67
  253.8 302.3 %collective-permute-start = (bf16[1,192,4096]{2,1,0:T(8,128)(2,1)}, bf16[1,192,4096]{2,1,0:T(8,128)(2,1)}, u32[]{:S(2)}, u32[]{:S(2)}) collective-permute-start(bf16[1,192,4096]{2,1,0:T(8,128)(2,1)} %param.15), channel_id=1, source_target_pairs={{0,128},{8,136},{16,144},{24,152},{32,160},{40,168},{48,176},{56,1... | collective-permute-start | bytes 4718600 | tf_op jit(solution)/shard_map/ppermute | solution.py:67
  392.5 5.4 copy-start.4
  392.5 86.2 %all-to-all-start.2 = ((bf16[8,32,4,512]{3,1,2,0:T(8,128)(2,1)}), bf16[8,32,4,512]{3,1,2,0:T(8,128)(2,1)S(1)}, u32[]{:S(2)}, u32[]{:S(2)}) async-start(bf16[8,32,4,512]{3,1,2,0:T(8,128)(2,1)} %copy.24), calls=%async_computation.2 | async-start | bytes 2097152 | tf_op jit(solution)/shard_map/all_to_all | solution.py:87
  480.9 87.6 %all-to-all-start.3 = ((bf16[32,4,4096]{2,1,0:T(4,128)(2,1)}), bf16[32,4,4096]{2,1,0:T(4,128)(2,1)S(1)}, u32[]{:S(2)}, u32[]{:S(2)}) async-start(bf16[32,4,4096]{2,1,0:T(4,128)(2,1)} %reshape.175), calls=%async_computation.3 | async-start | bytes 2097152 | tf_op jit(solution)/shard_map/all_to_all | solution.py:94
  525.1 33.7 %copy-start.3 = (bf16[1024,1536]{0,1:T(8,128)(2,1)S(1)}, bf16[1024,1536]{0,1:T(8,128)(2,1)}, u32[]{:S(2)}) copy-start(bf16[1024,1536]{0,1:T(8,128)(2,1)} %all-gather.4.cloned.1.call-done) | copy-start | bytes 9437188
  560.7 6.4 %collective-permute-start.3 = (f32[]{:T(128)}, f32[]{:T(128)}, u32[]{:S(2)}, u32[]{:S(2)}) collective-permute-start(f32[]{:T(128)} %convert_element_type.23), channel_id=1, source_target_pairs={{0,128},{8,136},{16,144},{24,152},{32,160},{40,168},{48,176},{56,1... | collective-permute-start | bytes 20 | tf_op jit(solution)/shard_map/ppermute | solution.py:105
Sparse Core Ops, SparseCore 0:
  46.9 173.0 all-gather.5
  244.8 140.3 all-gather.3

commit v3 on v2

--- a/solution.py
+++ b/solution.py
@@ -5,6 +5,7 @@
 
 TOPK = 8
 CAP = 4
+HALVES = 2
 
 
 def pair_partner(swap_pairs, device_count):
@@ -51,6 +52,10 @@
     return hidden.reshape(leading + (gate_local.shape[0],))
 
 
+def canonical(mine, theirs, first):
+    return jnp.stack([jnp.where(first, mine, theirs), jnp.where(first, theirs, mine)])
+
+
 def shards(
     tokens, expert_ids, gate_weights, expert_holder, swap_pairs, capacity, w_gate, w_up, w_down
 ):
@@ -59,11 +64,17 @@
     tok_rows, width = tokens.shape
     units = w_gate.shape[1]
     cols = width // replicas
+    ys = replicas // HALVES
     partner = pair_partner(swap_pairs, experts)
     me = lax.axis_index("expert")
     swapped = lax.dynamic_index_in_dim(partner, me, 0, keepdims=False) != me
     half = experts // 2
     ring = [(d, (d + half) % experts) for d in range(experts)]
+    rep = lax.axis_index("replica")
+    zh = rep // ys
+    first = zh == 0
+    across = [(q, (q + ys) % replicas) for q in range(replicas)]
+    ygroups = [[h * ys + j for j in range(ys)] for h in range(HALVES)]
     arrived = tuple(lax.ppermute(w, "expert", ring) for w in (w_gate, w_up, w_down))
     down_cols = lax.all_to_all(
         w_down[0].reshape(units, replicas, cols),
@@ -71,34 +82,57 @@
         split_axis=1,
         concat_axis=0,
         tiled=True,
-    ).reshape(units * replicas, cols)
-    slot_of, slot_kept, source, filled = route_slots(expert_ids, expert_holder, capacity)
-    outgoing = jnp.where(
-        filled[:, None], jnp.take(tokens, source, axis=0), jnp.zeros((), jnp.bfloat16)
+    ).reshape(replicas, units, cols)
+    blk_tokens = canonical(tokens, lax.ppermute(tokens, "replica", across), first)
+    blk_ids = canonical(expert_ids, lax.ppermute(expert_ids, "replica", across), first)
+    blk_gw = canonical(gate_weights, lax.ppermute(gate_weights, "replica", across), first)
+    slot_of, slot_kept, source, filled = jax.vmap(route_slots, in_axes=(0, None, None))(
+        blk_ids, expert_holder, capacity
     )
-    arrived_rows = lax.all_to_all(outgoing.reshape(experts, CAP, width), "expert", 0, 0, tiled=True)
-    group_rows = lax.all_gather(arrived_rows, "replica", axis=0, tiled=False)
+    picked = jax.vmap(lambda t, s: jnp.take(t, s, axis=0))(blk_tokens, source)
+    outgoing = jnp.where(filled[..., None], picked, jnp.zeros((), jnp.bfloat16))
+    outgoing = outgoing.reshape(HALVES, experts, CAP, width).transpose(1, 0, 2, 3)
+    arrived_rows = lax.all_to_all(outgoing, "expert", 0, 0, tiled=True)
+    group_rows = lax.all_gather(
+        arrived_rows, "replica", axis=0, tiled=False, axis_index_groups=ygroups
+    )
     hidden = expert_hidden(group_rows, w_gate[0], w_up[0]).reshape(-1, units)
-    hidden_all = lax.all_gather(hidden, "replica", axis=1, tiled=True)
+    pair_hidden = canonical(hidden, lax.ppermute(hidden, "replica", across), first)
+    hidden_all = lax.all_gather(
+        pair_hidden, "replica", axis=1, tiled=False, axis_index_groups=ygroups
+    ).reshape(replicas, -1, units)
     group_peak = jnp.max(jnp.abs(hidden_all)).astype(jnp.float32)
-    out_cols = jnp.dot(
-        hidden_all, down_cols, preferred_element_type=jnp.float32
+    out_cols = lax.dot_general(
+        hidden_all,
+        down_cols,
+        (((0, 2), (0, 1)), ((), ())),
+        preferred_element_type=jnp.float32,
     ).astype(jnp.bfloat16)
-    full_rows = lax.all_to_all(
-        out_cols.reshape(replicas, experts, CAP, cols),
+    half_rows = lax.all_to_all(
+        out_cols.reshape(ys, experts, HALVES, CAP, cols),
         "replica",
         split_axis=0,
-        concat_axis=3,
+        concat_axis=4,
         tiled=True,
+        axis_index_groups=ygroups,
     )
-    returned = lax.all_to_all(full_rows.reshape(experts, CAP, width), "expert", 0, 0, tiled=True)
-    fetched = jnp.take(returned.reshape(experts * CAP, width), slot_of, axis=0).reshape(
-        tok_rows, TOPK, width
+    returned = lax.all_to_all(
+        half_rows.reshape(experts, HALVES, CAP, ys * cols), "expert", 0, 0, tiled=True
     )
-    scales = jnp.where(slot_kept, gate_weights.reshape(-1), jnp.float32(0.0)).reshape(
-        tok_rows, TOPK, 1
+    by_block = returned.transpose(1, 0, 2, 3).reshape(HALVES, experts * CAP, ys * cols)
+    fetched = jax.vmap(lambda t, s: jnp.take(t, s, axis=0))(by_block, slot_of)
+    scales = jnp.where(slot_kept, blk_gw.reshape(HALVES, -1), jnp.float32(0.0))
+    combined = jnp.sum(
+        (scales[..., None] * fetched).reshape(HALVES, tok_rows, TOPK, ys * cols), axis=2
     )
-    moe_output = jnp.sum(scales * fetched, axis=1).astype(jnp.bfloat16)
+    own_half = jnp.where(first, combined[0], combined[1])
+    send_half = jnp.where(first, combined[1], combined[0])
+    recv_half = lax.ppermute(send_half, "replica", across)
+    moe_output = jnp.where(
+        first,
+        jnp.concatenate([own_half, recv_half], axis=1),
+        jnp.concatenate([recv_half, own_half], axis=1),
+    ).astype(jnp.bfloat16)
     moved_gate, moved_up, moved_down = (
         jnp.where(swapped, got, own) for got, own in zip(arrived, (w_gate, w_up, w_down))
     )

time: 585 us -> 524 us (0.90)
  waiting for transfers between devices: 444 us -> 317 us
  starting transfers between devices: 29.3 us -> 56.3 us
  blocking collectives: 34.9 us -> 54.6 us
  local copies, waits for them, and re-layouts: 24.1 us -> 42.1 us
  other arithmetic: 11.3 us -> 19.6 us
    all_gather x2, waiting for transfers between devices: 258 us -> 116 us  [the longest x1 82.8 us: shards(): lax.all_gather(arrived_rows, 'replica', axis=0, tiled=False, axis_index_g...]
    ppermute x0 -> x5, waiting for transfers between devices: none -> 94.3 us  [the longest x1 74 us: shards(): lax.ppermute(gate_weights, 'replica', across)]
    all_to_all x1, waiting for transfers between devices: 45.8 us -> 0.01 us  [shards(): lax.all_to_all(w_down[0].reshape(units, replicas, cols), 'replica', split...]
    ppermute x3, waiting for transfers between devices: 136 us -> 94.4 us  [shards(): lax.ppermute(w, 'expert', ring)]
    ppermute x0 -> x5, starting transfers between devices: none -> 24.8 us  [the longest x1 7.28 us: shards(): lax.ppermute(tokens, 'replica', across)]
    all_to_all x1, blocking collectives: 34.9 us -> 54.6 us  [shards(): arrived_rows = lax.all_to_all(outgoing, 'expert', 0, 0, tiled=True)]
    all_to_all x1, starting transfers between devices: 3.71 us -> 13.9 us  [shards(): lax.all_to_all(w_down[0].reshape(units, replicas, cols), 'replica', split...]
    gather x3 -> x4, local copies, waits for them, and re-layouts: 2.48 us -> 11.9 us  [the longest x2 9.37 us: shards(): picked = jax.vmap(lambda t, s: jnp.take(t, s, axis=0))(blk_tokens, source)]
  transfers between devices with their start and end apart: 9 -> 14, of which waited for: 7 -> 10; matrix products, arithmetic and copies ran while one was open for 4% -> 7% of each run, Pallas kernels for 0% -> 0%
where the time goes in v3:
time: 524 us; the launch traced here: 523 us
  waiting for transfers between devices  317 us (60%)
  starting transfers between devices  56.3 us (11%)
  blocking collectives  54.6 us (10%)
  local copies, waits for them, and re-layouts  42.1 us (8%)
  other arithmetic  19.6 us (4%)
  between operations  17.9 us (3%)
  matrix products  15.5 us (3%)
    ppermute x3, waiting for transfers between devices, shards(): lax.ppermute(w, 'expert', ring)  94.4 us
    all_gather x1, waiting for transfers between devices, shards(): lax.all_gather(arrived_rows, 'replica', axis=0, tiled=False, axis_index_g...  82.8 us
    ppermute x1, waiting for transfers between devices, shards(): lax.ppermute(gate_weights, 'replica', across)  74 us
    all_to_all x1, blocking collectives, shards(): arrived_rows = lax.all_to_all(outgoing, 'expert', 0, 0, tiled=True)  54.6 us
    all_gather x1, waiting for transfers between devices, shards(): lax.all_gather(pair_hidden, 'replica', axis=1, tiled=False, axis_index_gr...  33.4 us
    all_to_all x1, starting transfers between devices, shards(): lax.all_to_all(w_down[0].reshape(units, replicas, cols), 'replica', split...  13.9 us
    ppermute x1, waiting for transfers between devices, shards(): lax.ppermute(hidden, 'replica', across)  12.7 us
    reshape x1, local copies, waits for them, and re-layouts, expert_hidden(): row_matrix = row_block.reshape(-1, row_block.shape[-1])  12.5 us
  transfers between devices with their start and end apart: 14, of which 10 were waited for; matrix products, arithmetic and copies ran while one was open for 7% of the time, Pallas kernels for 0%

profile of v3, /device:TPU:2, one launch (start us, length us, event | category | flops | bytes accessed | tf_op | source)
XLA Modules:
  0.0 522.6 jit_solution(15501993207551101365)
XLA Ops:
  7.2 7.3 %collective-permute-start.2 = (bf16[8,4096]{1,0:T(8,128)(2,1)}, bf16[8,4096]{1,0:T(8,128)(2,1)S(1)}, u32[]{:S(2)}, u32[]{:S(2)}) collective-permute-start(bf16[8,4096]{1,0:T(8,128)(2,1)} %param.9), channel_id=1, source_target_pairs={{0,4},{1,5},{2,6},{3,7},{4,0},{5,1},{6,2},{7,3},{8,12},{9,13},{10,... | collective-permute-start | bytes 196616 | tf_op jit(solution)/shard_map/ppermute | solution.py:86
  14.6 7.7 %collective-permute-done = s32[8,8]{1,0:T(8,128)S(1)} collective-permute-done((s32[8,8]{1,0:T(8,128)}, s32[8,8]{1,0:T(8,128)S(1)}, u32[]{:S(2)}, u32[]{:S(2)}) %collective-permute-start) | collective-permute-done | bytes 288 | tf_op jit(solution)/shard_map/ppermute | solution.py:87
  25.7 7.2 %gather_fusion = bf16[256,4096]{1,0:T(8,128)(2,1)S(1)} fusion(bf16[2,8,4096]{2,1,0:T(8,128)(2,1)S(1)} %pad_maximum_fusion.1, s32[256]{0:T(256)S(1)} %fusion.20), kind=kCustom, calls=%fused_computation | custom fusion | bytes 4196352 | tf_op jit(solution)/shard_map/vmap(jit(_take))/gather | solution.py:92
  37.8 54.6 %all_to_all.40 = bf16[32,2,4,4096]{3,2,1,0:T(4,128)(2,1)} all-to-all(bf16[32,2,4,4096]{3,2,1,0:T(4,128)(2,1)S(1)} %fusion.1), channel_id=1, replica_groups=mesh['expert'=32,'replica'=8] {'expert'}, dimensions={0} | all-to-all | bytes 4194304 | tf_op jit(solution)/shard_map/all_to_all | solution.py:95
  92.6 82.8 %all-gather.5.cloned.1.call-done = bf16[128,2,4,4096]{3,2,1,0:T(4,128)(2,1)} async-done(((bf16[32,2,4,4096]{3,2,1,0:T(4,128)(2,1)}), bf16[128,2,4,4096]{3,2,1,0:T(4,128)(2,1)}) %all-gather.5.cloned.1.call-update) | async-done | bytes 8388624 | tf_op jit(solution)/shard_map/all_gather | solution.py:96
  175.4 12.5 %reshape.161 = bf16[1024,4096]{1,0:T(8,128)(2,1)} reshape(bf16[128,2,4,4096]{3,2,1,0:T(4,128)(2,1)} %all-gather.5.cloned.1.call-done) | data formatting | bytes 16777216 | tf_op jit(solution)/shard_map/reshape | solution.py:45
  187.9 6.8 %fusion.5 = f32[1024,192]{0,1:T(8,128)S(1)} fusion(bf16[1024,4096]{1,0:T(8,128)(2,1)} %reshape.161, bf16[1,192,4096]{2,1,0:T(8,128)(2,1)} %param.15), kind=kOutput, calls=%fused_computation.10 | convolution fusion | flops 1610612736 | bytes 10747904 | tf_op jit(solution)/shard_map/dot_general | solution.py:47
  194.8 4.4 fusion.11
  199.1 5.8 %collective-permute-start.3 = (bf16[1024,192]{0,1:T(8,128)(2,1)S(1)}, bf16[1024,192]{0,1:T(8,128)(2,1)S(1)}, u32[]{:S(2)}, u32[]{:S(2)}) collective-permute-start(bf16[1024,192]{0,1:T(8,128)(2,1)S(1)} %fusion.11), channel_id=1, source_target_pairs={{0,4},{1,5},{2,6},{3,7},{4,0},{5,1},{6,2},{7,3},{8,12},{9,13},{10,... | collective-permute-start | bytes 1179656 | tf_op jit(solution)/shard_map/ppermute | solution.py:100
  205.0 12.7 %collective-permute-done.3 = bf16[1024,192]{0,1:T(8,128)(2,1)S(1)} collective-permute-done((bf16[1024,192]{0,1:T(8,128)(2,1)S(1)}, bf16[1024,192]{0,1:T(8,128)(2,1)S(1)}, u32[]{:S(2)}, u32[]{:S(2)}) %collective-permute-start.3) | collective-permute-done | bytes 393248 | tf_op jit(solution)/shard_map/ppermute | solution.py:100
  222.4 13.9 %all-to-all-start.1 = ((bf16[192,8,512]{2,0,1:T(8,128)(2,1)}), bf16[192,8,512]{2,0,1:T(8,128)(2,1)}, u32[]{:S(2)}, u32[]{:S(2)}) async-start(bf16[192,8,512]{2,0,1:T(8,128)(2,1)} %copy.44), calls=%async_computation.1 | async-start | bytes 3145728 | tf_op jit(solution)/shard_map/all_to_all | solution.py:79
  239.8 5.9 %collective-permute-start.1 = (f32[8,8]{1,0:T(8,128)S(1)}, f32[8,8]{1,0:T(8,128)S(1)}, u32[]{:S(2)}, u32[]{:S(2)}) collective-permute-start(f32[8,8]{1,0:T(8,128)S(1)} %copy-done.1), channel_id=1, source_target_pairs={{0,4},{1,5},{2,6},{3,7},{4,0},{5,1},{6,2},{7,3},{8,12},{9,13},{10,... | collective-permute-start | bytes 776 | tf_op jit(solution)/shard_map/ppermute | solution.py:88
  245.8 33.4 %all-gather.7.cloned.1.call-done = bf16[2,4096,192]{1,2,0:T(8,128)(2,1)} async-done(((bf16[2,1024,192]{1,2,0:T(8,128)(2,1)}), bf16[2,4096,192]{1,2,0:T(8,128)(2,1)}) %all-gather.7.cloned.1.call-update) | async-done | bytes 3145744 | tf_op jit(solution)/shard_map/all_gather | solution.py:101
  279.2 5.2 copy.43
  287.3 4.3 bitcast_convert_fusion
  293.2 3.5 all-to-all-start.2
  298.0 74.0 %collective-permute-done.1 = f32[8,8]{1,0:T(8,128)S(1)} collective-permute-done((f32[8,8]{1,0:T(8,128)S(1)}, f32[8,8]{1,0:T(8,128)S(1)}, u32[]{:S(2)}, u32[]{:S(2)}) %collective-permute-start.1) | collective-permute-done | bytes 288 | tf_op jit(solution)/shard_map/ppermute | solution.py:88
  374.6 8.9 %all-to-all-start.3 = ((bf16[32,2,4,2048]{3,2,1,0:T(4,128)(2,1)}), bf16[32,2,4,2048]{3,2,1,0:T(4,128)(2,1)S(1)}, u32[]{:S(2)}, u32[]{:S(2)}) async-start(bf16[32,2,4,2048]{3,2,1,0:T(4,128)(2,1)} %reshape.193), calls=%async_computation.3 | async-start | bytes 2097152 | tf_op jit(solution)/shard_map/all_to_all | solution.py:119
  383.5 32.5 %collective-permute-done.7 = bf16[1,192,4096]{2,1,0:T(8,128)(2,1)} collective-permute-done((bf16[1,192,4096]{2,1,0:T(8,128)(2,1)}, bf16[1,192,4096]{2,1,0:T(8,128)(2,1)}, u32[]{:S(2)}, u32[]{:S(2)}) %collective-permute-start.7) | collective-permute-done | bytes 1572896 | tf_op jit(solution)/shard_map/ppermute | solution.py:78
  418.7 31.0 %collective-permute-done.6 = bf16[1,192,4096]{2,1,0:T(8,128)(2,1)} collective-permute-done((bf16[1,192,4096]{2,1,0:T(8,128)(2,1)}, bf16[1,192,4096]{2,1,0:T(8,128)(2,1)}, u32[]{:S(2)}, u32[]{:S(2)}) %collective-permute-start.6) | collective-permute-done | bytes 1572896 | tf_op jit(solution)/shard_map/ppermute | solution.py:78
  452.4 31.0 %collective-permute-done.5 = bf16[1,192,4096]{2,1,0:T(8,128)(2,1)} collective-permute-done((bf16[1,192,4096]{2,1,0:T(8,128)(2,1)}, bf16[1,192,4096]{2,1,0:T(8,128)(2,1)}, u32[]{:S(2)}, u32[]{:S(2)}) %collective-permute-start.5) | collective-permute-done | bytes 1572896 | tf_op jit(solution)/shard_map/ppermute | solution.py:78
  486.1 8.3 %all-to-all-done.3 = bf16[32,2,4,2048]{3,2,1,0:T(4,128)(2,1)S(1)} async-done(((bf16[32,2,4,2048]{3,2,1,0:T(4,128)(2,1)}), bf16[32,2,4,2048]{3,2,1,0:T(4,128)(2,1)S(1)}, u32[]{:S(2)}, u32[]{:S(2)}) %all-to-all-start.3) | async-done | bytes 1048608 | tf_op jit(solution)/shard_map/all_to_all | solution.py:119
  498.8 5.7 %collective-permute-start.4 = (bf16[8,2048]{1,0:T(8,128)(2,1)S(1)}, bf16[8,2048]{1,0:T(8,128)(2,1)S(1)}, u32[]{:S(2)}, u32[]{:S(2)}) collective-permute-start(bf16[8,2048]{1,0:T(8,128)(2,1)S(1)} %get-tuple-element.17), channel_id=1, source_target_pairs={{0,4},{1,5},{2,6},{3,7},{4,0},{5,1},{6,2},{7,3},{8,12},{9,13},{10,... | collective-permute-start | bytes 98312 | tf_op jit(solution)/shard_map/ppermute | solution.py:130
  509.5 3.3 collective-permute-done.8
  (69 shorter events, 42.1 us)
Async XLA Ops:
  7.2 168.2 %all-gather.5.cloned.1.call-start = ((), (), s32[]{:S(2)}) async-start(), calls=%async_computation.4 | async-start | bytes 10485760 | tf_op jit(solution)/shard_map/all_gather | solution.py:96
  7.2 17.6 %collective-permute-start.2 = (bf16[8,4096]{1,0:T(8,128)(2,1)}, bf16[8,4096]{1,0:T(8,128)(2,1)S(1)}, u32[]{:S(2)}, u32[]{:S(2)}) collective-permute-start(bf16[8,4096]{1,0:T(8,128)(2,1)} %param.9), channel_id=1, source_target_pairs={{0,4},{1,5},{2,6},{3,7},{4,0},{5,1},{6,2},{7,3},{8,12},{9,13},{10,... | collective-permute-start | bytes 196616 | tf_op jit(solution)/shard_map/ppermute | solution.py:86
  14.5 7.8 %collective-permute-start = (s32[8,8]{1,0:T(8,128)}, s32[8,8]{1,0:T(8,128)S(1)}, u32[]{:S(2)}, u32[]{:S(2)}) collective-permute-start(s32[8,8]{1,0:T(8,128)} %param.10), channel_id=1, source_target_pairs={{0,4},{1,5},{2,6},{3,7},{4,0},{5,1},{6,2},{7,3},{8,12},{9,13},{10,... | collective-permute-start | bytes 776 | tf_op jit(solution)/shard_map/ppermute | solution.py:87
  92.4 186.8 %all-gather.7.cloned.1.call-start = ((), (), s32[]{:S(2)}) async-start(), calls=%async_computation.5 | async-start | bytes 3932160 | tf_op jit(solution)/shard_map/all_gather | solution.py:101
  187.9 6.8 %copy-start = (bf16[1024,4096]{1,0:T(8,128)(2,1)S(1)}, bf16[1024,4096]{1,0:T(8,128)(2,1)}, u32[]{:S(2)}) copy-start(bf16[1024,4096]{1,0:T(8,128)(2,1)} %reshape.161) | copy-start | bytes 25165828
  199.1 18.5 %collective-permute-start.3 = (bf16[1024,192]{0,1:T(8,128)(2,1)S(1)}, bf16[1024,192]{0,1:T(8,128)(2,1)S(1)}, u32[]{:S(2)}, u32[]{:S(2)}) collective-permute-start(bf16[1024,192]{0,1:T(8,128)(2,1)S(1)} %fusion.11), channel_id=1, source_target_pairs={{0,4},{1,5},{2,6},{3,7},{4,0},{5,1},{6,2},{7,3},{8,12},{9,13},{10,... | collective-permute-start | bytes 1179656 | tf_op jit(solution)/shard_map/ppermute | solution.py:100
  222.4 17.4 %copy-start.1 = (f32[8,8]{1,0:T(8,128)S(1)}, f32[8,8]{1,0:T(8,128)}, u32[]{:S(2)}) copy-start(f32[8,8]{1,0:T(8,128)} %param.11) | copy-start | bytes 772
  222.4 23.3 %copy-start.2 = (s32[8,2]{0,1:T(2,128)S(1)}, s32[8,2]{0,1:T(2,128)}, u32[]{:S(2)}) copy-start(s32[8,2]{0,1:T(2,128)} %param.13) | copy-start | bytes 196
  222.4 65.0 %all-to-all-start.1 = ((bf16[192,8,512]{2,0,1:T(8,128)(2,1)}), bf16[192,8,512]{2,0,1:T(8,128)(2,1)}, u32[]{:S(2)}, u32[]{:S(2)}) async-start(bf16[192,8,512]{2,0,1:T(8,128)(2,1)} %copy.44), calls=%async_computation.1 | async-start | bytes 3145728 | tf_op jit(solution)/shard_map/all_to_all | solution.py:79
  236.3 179.7 %collective-permute-start.7 = (bf16[1,192,4096]{2,1,0:T(8,128)(2,1)}, bf16[1,192,4096]{2,1,0:T(8,128)(2,1)}, u32[]{:S(2)}, u32[]{:S(2)}) collective-permute-start(bf16[1,192,4096]{2,1,0:T(8,128)(2,1)} %param.17), channel_id=1, source_target_pairs={{0,128},{8,136},{16,144},{24,152},{32,160},{40,168},{48,176},{56,1... | collective-permute-start | bytes 4718600 | tf_op jit(solution)/shard_map/ppermute | solution.py:78
  236.8 212.9 %collective-permute-start.6 = (bf16[1,192,4096]{2,1,0:T(8,128)(2,1)}, bf16[1,192,4096]{2,1,0:T(8,128)(2,1)}, u32[]{:S(2)}, u32[]{:S(2)}) collective-permute-start(bf16[1,192,4096]{2,1,0:T(8,128)(2,1)} %param.16), channel_id=1, source_target_pairs={{0,128},{8,136},{16,144},{24,152},{32,160},{40,168},{48,176},{56,1... | collective-permute-start | bytes 4718600 | tf_op jit(solution)/shard_map/ppermute | solution.py:78
  239.3 244.1 %collective-permute-start.5 = (bf16[1,192,4096]{2,1,0:T(8,128)(2,1)}, bf16[1,192,4096]{2,1,0:T(8,128)(2,1)}, u32[]{:S(2)}, u32[]{:S(2)}) collective-permute-start(bf16[1,192,4096]{2,1,0:T(8,128)(2,1)} %param.15), channel_id=1, source_target_pairs={{0,128},{8,136},{16,144},{24,152},{32,160},{40,168},{48,176},{56,1... | collective-permute-start | bytes 4718600 | tf_op jit(solution)/shard_map/ppermute | solution.py:78
  239.8 132.2 %collective-permute-start.1 = (f32[8,8]{1,0:T(8,128)S(1)}, f32[8,8]{1,0:T(8,128)S(1)}, u32[]{:S(2)}, u32[]{:S(2)}) collective-permute-start(f32[8,8]{1,0:T(8,128)S(1)} %copy-done.1), channel_id=1, source_target_pairs={{0,4},{1,5},{2,6},{3,7},{4,0},{5,1},{6,2},{7,3},{8,12},{9,13},{10,... | collective-permute-start | bytes 776 | tf_op jit(solution)/shard_map/ppermute | solution.py:88
  293.2 79.0 %all-to-all-start.2 = ((bf16[4,32,2,4,512]{4,1,3,2,0:T(8,128)(2,1)}), bf16[4,32,2,4,512]{4,1,3,2,0:T(8,128)(2,1)S(1)}, u32[]{:S(2)}, u32[]{:S(2)}) async-start(bf16[4,32,2,4,512]{4,1,3,2,0:T(8,128)(2,1)} %copy.46), calls=%async_computation.2 | async-start | bytes 2097152 | tf_op jit(solution)/shard_map/all_to_all | solution.py:111
  374.6 119.9 %all-to-all-start.3 = ((bf16[32,2,4,2048]{3,2,1,0:T(4,128)(2,1)}), bf16[32,2,4,2048]{3,2,1,0:T(4,128)(2,1)S(1)}, u32[]{:S(2)}, u32[]{:S(2)}) async-start(bf16[32,2,4,2048]{3,2,1,0:T(4,128)(2,1)} %reshape.193), calls=%async_computation.3 | async-start | bytes 2097152 | tf_op jit(solution)/shard_map/all_to_all | solution.py:119
  498.8 15.1 %collective-permute-start.4 = (bf16[8,2048]{1,0:T(8,128)(2,1)S(1)}, bf16[8,2048]{1,0:T(8,128)(2,1)S(1)}, u32[]{:S(2)}, u32[]{:S(2)}) collective-permute-start(bf16[8,2048]{1,0:T(8,128)(2,1)S(1)} %get-tuple-element.17), channel_id=1, source_target_pairs={{0,4},{1,5},{2,6},{3,7},{4,0},{5,1},{6,2},{7,3},{8,12},{9,13},{10,... | collective-permute-start | bytes 98312 | tf_op jit(solution)/shard_map/ppermute | solution.py:130
  508.1 4.7 collective-permute-start.8
Sparse Core Ops, SparseCore 0:
  92.5 82.8 all-gather.4
  218.8 60.3 all-gather.6

commit v4 on v3

--- a/solution.py
+++ b/solution.py
@@ -6,6 +6,7 @@
 TOPK = 8
 CAP = 4
 HALVES = 2
+PLANES = 4
 
 
 def pair_partner(swap_pairs, device_count):
@@ -65,8 +66,11 @@
     units = w_gate.shape[1]
     cols = width // replicas
     ys = replicas // HALVES
+    plane = experts // PLANES
+    blocks = PLANES * HALVES
     partner = pair_partner(swap_pairs, experts)
     me = lax.axis_index("expert")
+    zl = me // plane
     swapped = lax.dynamic_index_in_dim(partner, me, 0, keepdims=False) != me
     half = experts // 2
     ring = [(d, (d + half) % experts) for d in range(experts)]
@@ -75,6 +79,8 @@
     first = zh == 0
     across = [(q, (q + ys) % replicas) for q in range(replicas)]
     ygroups = [[h * ys + j for j in range(ys)] for h in range(HALVES)]
+    zgroups = [[p * plane + c for p in range(PLANES)] for c in range(plane)]
+    pgroups = [[p * plane + c for c in range(plane)] for p in range(PLANES)]
     arrived = tuple(lax.ppermute(w, "expert", ring) for w in (w_gate, w_up, w_down))
     down_cols = lax.all_to_all(
         w_down[0].reshape(units, replicas, cols),
@@ -83,16 +89,30 @@
         concat_axis=0,
         tiled=True,
     ).reshape(replicas, units, cols)
-    blk_tokens = canonical(tokens, lax.ppermute(tokens, "replica", across), first)
-    blk_ids = canonical(expert_ids, lax.ppermute(expert_ids, "replica", across), first)
-    blk_gw = canonical(gate_weights, lax.ppermute(gate_weights, "replica", across), first)
+    pair_tokens = canonical(tokens, lax.ppermute(tokens, "replica", across), first)
+    pair_ids = canonical(expert_ids, lax.ppermute(expert_ids, "replica", across), first)
+    pair_gw = canonical(gate_weights, lax.ppermute(gate_weights, "replica", across), first)
+    blk_tokens, blk_ids, blk_gw = (
+        lax.all_gather(v, "expert", axis=0, tiled=True, axis_index_groups=zgroups)
+        for v in (pair_tokens, pair_ids, pair_gw)
+    )
     slot_of, slot_kept, source, filled = jax.vmap(route_slots, in_axes=(0, None, None))(
         blk_ids, expert_holder, capacity
     )
+    lo = zl * (plane * CAP)
+    source = lax.dynamic_slice_in_dim(source, lo, plane * CAP, axis=1)
+    filled = lax.dynamic_slice_in_dim(filled, lo, plane * CAP, axis=1)
     picked = jax.vmap(lambda t, s: jnp.take(t, s, axis=0))(blk_tokens, source)
     outgoing = jnp.where(filled[..., None], picked, jnp.zeros((), jnp.bfloat16))
-    outgoing = outgoing.reshape(HALVES, experts, CAP, width).transpose(1, 0, 2, 3)
-    arrived_rows = lax.all_to_all(outgoing, "expert", 0, 0, tiled=True)
+    outgoing = outgoing.reshape(blocks, plane, CAP, width).transpose(1, 0, 2, 3)
+    arrived_rows = lax.all_to_all(
+        outgoing.reshape(plane, blocks * CAP, width),
+        "expert",
+        0,
+        0,
+        tiled=True,
+        axis_index_groups=pgroups,
+    )
     group_rows = lax.all_gather(
         arrived_rows, "replica", axis=0, tiled=False, axis_index_groups=ygroups
     )
@@ -109,22 +129,39 @@
         preferred_element_type=jnp.float32,
     ).astype(jnp.bfloat16)
     half_rows = lax.all_to_all(
-        out_cols.reshape(ys, experts, HALVES, CAP, cols),
+        out_cols.reshape(ys, plane, blocks * CAP, cols),
         "replica",
         split_axis=0,
-        concat_axis=4,
+        concat_axis=3,
         tiled=True,
         axis_index_groups=ygroups,
     )
     returned = lax.all_to_all(
-        half_rows.reshape(experts, HALVES, CAP, ys * cols), "expert", 0, 0, tiled=True
-    )
-    by_block = returned.transpose(1, 0, 2, 3).reshape(HALVES, experts * CAP, ys * cols)
-    fetched = jax.vmap(lambda t, s: jnp.take(t, s, axis=0))(by_block, slot_of)
-    scales = jnp.where(slot_kept, blk_gw.reshape(HALVES, -1), jnp.float32(0.0))
-    combined = jnp.sum(
-        (scales[..., None] * fetched).reshape(HALVES, tok_rows, TOPK, ys * cols), axis=2
-    )
+        half_rows.reshape(plane, blocks * CAP, ys * cols),
+        "expert",
+        0,
+        0,
+        tiled=True,
+        axis_index_groups=pgroups,
+    )
+    by_block = returned.reshape(plane, blocks, CAP, ys * cols).transpose(1, 0, 2, 3)
+    by_block = by_block.reshape(blocks, plane * CAP, ys * cols)
+    in_plane = (slot_of // (plane * CAP)) == zl
+    local_slot = slot_of % (plane * CAP)
+    fetched = jax.vmap(lambda t, s: jnp.take(t, s, axis=0))(by_block, local_slot)
+    scales = jnp.where(slot_kept & in_plane, blk_gw.reshape(blocks, -1), jnp.float32(0.0))
+    partial_sum = jnp.sum(
+        (scales[..., None] * fetched).reshape(blocks, tok_rows, TOPK, ys * cols), axis=2
+    )
+    summed = lax.all_to_all(
+        partial_sum.reshape(PLANES, HALVES, tok_rows, ys * cols),
+        "expert",
+        0,
+        0,
+        tiled=True,
+        axis_index_groups=zgroups,
+    )
+    combined = jnp.sum(summed, axis=0)
     own_half = jnp.where(first, combined[0], combined[1])
     send_half = jnp.where(first, combined[1], combined[0])
     recv_half = lax.ppermute(send_half, "replica", across)

time: 524 us -> 585 us (1.12)
  blocking collectives: 54.6 us -> 164 us
  waiting for transfers between devices: 317 us -> 261 us
  other arithmetic: 19.6 us -> 25.9 us
    all_gather x0 -> x3, blocking collectives: none -> 133 us  [shards(): lax.all_gather(v, 'expert', axis=0, tiled=True, axis_index_groups=zgroups)]
    ppermute x3, waiting for transfers between devices: 94.4 us -> 0.01 us  [shards(): lax.ppermute(w, 'expert', ring)]
    ppermute x1, waiting for transfers between devices: 74 us -> 125 us  [shards(): lax.ppermute(gate_weights, 'replica', across)]
    all_gather x1, waiting for transfers between devices: 33.4 us -> 0.02 us  [shards(): lax.all_gather(pair_hidden, 'replica', axis=1, tiled=False, axis_index_gr...]
    all_to_all x2 -> x3, waiting for transfers between devices: 8.32 us -> 33.9 us  [the longest x1 11.7 us: shards(): lax.all_to_all(half_rows.reshape(plane, blocks * CAP, ys * cols), 'expert...]
    all_to_all x1, blocking collectives: 54.6 us -> 30.7 us  [shards(): lax.all_to_all(outgoing.reshape(plane, blocks * CAP, width), 'expert', 0,...]
    reshape x6 -> x3, local copies, waits for them, and re-layouts: 16.7 us -> 3.02 us  [the longest x1 1.59 us: shards(): half_rows.reshape(plane, blocks * CAP, ys * cols)]
    ppermute x1, starting transfers between devices: 0.1 us -> 7.28 us  [shards(): lax.ppermute(expert_ids, 'replica', across)]
  transfers between devices with their start and end apart: 14 -> 15, of which waited for: 10 -> 8; matrix products, arithmetic and copies ran while one was open for 7% -> 8% of each run, Pallas kernels for 0% -> 0%
where the time goes in v4:
time: 585 us; the launch traced here: 581 us
  waiting for transfers between devices  261 us (45%)
  blocking collectives  164 us (28%)
  starting transfers between devices  58.5 us (10%)
  local copies, waits for them, and re-layouts  36.4 us (6%)
  other arithmetic  25.9 us (4%)
  between operations  18.3 us (3%)
  matrix products  16.5 us (3%)
    all_gather x3, blocking collectives, shards(): lax.all_gather(v, 'expert', axis=0, tiled=True, axis_index_groups=zgroups)  133 us
    ppermute x1, waiting for transfers between devices, shards(): lax.ppermute(gate_weights, 'replica', across)  125 us
    all_gather x1, waiting for transfers between devices, shards(): lax.all_gather(arrived_rows, 'replica', axis=0, tiled=False, axis_index_g...  85.2 us
    all_to_all x1, blocking collectives, shards(): lax.all_to_all(outgoing.reshape(plane, blocks * CAP, width), 'expert', 0,...  30.7 us
    all_to_all x1, starting transfers between devices, shards(): lax.all_to_all(w_down[0].reshape(units, replicas, cols), 'replica', split...  13.9 us
    ppermute x1, waiting for transfers between devices, shards(): lax.ppermute(hidden, 'replica', across)  12.7 us
  transfers between devices with their start and end apart: 15, of which 8 were waited for; matrix products, arithmetic and copies ran while one was open for 8% of the time, Pallas kernels for 0%

profile of v4, /device:TPU:2, one launch (start us, length us, event | category | flops | bytes accessed | tf_op | source)
XLA Modules:
  0.0 580.7 jit_solution(4612762519950626800)
XLA Ops:
  7.2 7.3 %collective-permute-start = (s32[8,8]{1,0:T(8,128)}, s32[8,8]{1,0:T(8,128)S(1)}, u32[]{:S(2)}, u32[]{:S(2)}) collective-permute-start(s32[8,8]{1,0:T(8,128)} %param.10), channel_id=1, source_target_pairs={{0,4},{1,5},{2,6},{3,7},{4,0},{5,1},{6,2},{7,3},{8,12},{9,13},{10,... | collective-permute-start | bytes 776 | tf_op jit(solution)/shard_map/ppermute | solution.py:93
  17.0 13.1 %all_gather.21 = s32[8,8,8]{2,1,0:T(8,128)S(1)} all-gather(s32[2,8,8]{2,1,0:T(8,128)S(1)} %pad_add_fusion), channel_id=1, replica_groups={{0,64,128,192},{8,72,136,200},{16,80,144,208},{24,88,152,216},{32,96,16..., dimensions={0}, use_global_device_ids=true | all-gather | bytes 2560 | tf_op jit(solution)/shard_map/all_gather | solution.py:96
  36.5 16.2 %all_gather.23 = bf16[8,8,4096]{2,1,0:T(8,128)(2,1)S(1)} all-gather(bf16[2,8,4096]{2,1,0:T(8,128)(2,1)S(1)} %pad_maximum_fusion.1), channel_id=1, replica_groups={{0,64,128,192},{8,72,136,200},{16,80,144,208},{24,88,152,216},{32,96,16..., dimensions={0}, use_global_device_ids=true | all-gather | bytes 655360 | tf_op jit(solution)/shard_map/all_gather | solution.py:96
  52.7 7.1 %gather_fusion = bf16[256,4096]{1,0:T(8,128)(2,1)S(1)} fusion(bf16[8,8,4096]{2,1,0:T(8,128)(2,1)S(1)} %all_gather.23, s32[256]{0:T(256)S(1)} %reshape.189), kind=kCustom, calls=%fused_computation | custom fusion | bytes 4196352 | tf_op jit(solution)/shard_map/vmap(jit(_take))/gather | solution.py:105
  67.5 30.7 %all_to_all.45 = bf16[8,32,4096]{2,1,0:T(8,128)(2,1)} all-to-all(bf16[8,32,4096]{2,1,0:T(8,128)(2,1)S(1)} %copy.95), channel_id=1, replica_groups={{0,8,16,24,32,40,48,56},{64,72,80,88,96,104,112,120},{128,136,144,152,1..., dimensions={0} | all-to-all | bytes 4194304 | tf_op jit(solution)/shard_map/all_to_all | solution.py:108
  98.8 85.2 %all-gather.5.cloned.1.call-done = bf16[32,32,4096]{2,1,0:T(8,128)(2,1)} async-done(((bf16[8,32,4096]{2,1,0:T(8,128)(2,1)}), bf16[32,32,4096]{2,1,0:T(8,128)(2,1)}) %all-gather.5.cloned.1.call-update) | async-done | bytes 8388624 | tf_op jit(solution)/shard_map/all_gather | solution.py:116
  183.9 6.8 %fusion.4 = f32[1024,192]{0,1:T(8,128)S(1)} fusion(bf16[1024,4096]{1,0:T(8,128)(2,1)} %bitcast.102, bf16[1,192,4096]{2,1,0:T(8,128)(2,1)} %param.15), kind=kOutput, calls=%fused_computation.10 | convolution fusion | flops 1610612736 | bytes 10747904 | tf_op jit(solution)/shard_map/dot_general | solution.py:48
  190.8 4.4 fusion.10
  195.2 5.8 %collective-permute-start.3 = (bf16[1024,192]{0,1:T(8,128)(2,1)S(1)}, bf16[1024,192]{0,1:T(8,128)(2,1)S(1)}, u32[]{:S(2)}, u32[]{:S(2)}) collective-permute-start(bf16[1024,192]{0,1:T(8,128)(2,1)S(1)} %fusion.10), channel_id=1, source_target_pairs={{0,4},{1,5},{2,6},{3,7},{4,0},{5,1},{6,2},{7,3},{8,12},{9,13},{10,... | collective-permute-start | bytes 1179656 | tf_op jit(solution)/shard_map/ppermute | solution.py:120
  201.0 12.7 %collective-permute-done.3 = bf16[1024,192]{0,1:T(8,128)(2,1)S(1)} collective-permute-done((bf16[1024,192]{0,1:T(8,128)(2,1)S(1)}, bf16[1024,192]{0,1:T(8,128)(2,1)S(1)}, u32[]{:S(2)}, u32[]{:S(2)}) %collective-permute-start.3) | collective-permute-done | bytes 393248 | tf_op jit(solution)/shard_map/ppermute | solution.py:120
  218.4 13.9 %all-to-all-start.1 = ((bf16[192,8,512]{2,0,1:T(8,128)(2,1)}), bf16[192,8,512]{2,0,1:T(8,128)(2,1)}, u32[]{:S(2)}, u32[]{:S(2)}) async-start(bf16[192,8,512]{2,0,1:T(8,128)(2,1)} %copy.97), calls=%async_computation.1 | async-start | bytes 3145728 | tf_op jit(solution)/shard_map/all_to_all | solution.py:85
  235.8 5.9 %collective-permute-start.1 = (f32[8,8]{1,0:T(8,128)S(1)}, f32[8,8]{1,0:T(8,128)S(1)}, u32[]{:S(2)}, u32[]{:S(2)}) collective-permute-start(f32[8,8]{1,0:T(8,128)S(1)} %copy-done.1), channel_id=1, source_target_pairs={{0,4},{1,5},{2,6},{3,7},{4,0},{5,1},{6,2},{7,3},{8,12},{9,13},{10,... | collective-permute-start | bytes 776 | tf_op jit(solution)/shard_map/ppermute | solution.py:94
  243.4 124.6 %collective-permute-done.1 = f32[8,8]{1,0:T(8,128)S(1)} collective-permute-done((f32[8,8]{1,0:T(8,128)S(1)}, f32[8,8]{1,0:T(8,128)S(1)}, u32[]{:S(2)}, u32[]{:S(2)}) %collective-permute-start.1) | collective-permute-done | bytes 288 | tf_op jit(solution)/shard_map/ppermute | solution.py:94
  368.0 103.8 %all_gather.22 = f32[8,8,8]{2,1,0:T(8,128)S(1)} all-gather(f32[2,8,8]{2,1,0:T(8,128)S(1)} %pad_maximum_fusion.2), channel_id=1, replica_groups={{0,64,128,192},{8,72,136,200},{16,80,144,208},{24,88,152,216},{32,96,16..., dimensions={0}, use_global_device_ids=true | all-gather | bytes 2560 | tf_op jit(solution)/shard_map/all_gather | solution.py:96
  471.9 5.2 copy.96
  480.1 5.3 bitcast_convert_fusion
  485.3 4.5 all-to-all-start.2
  492.6 10.8 %all-to-all-done.2 = bf16[4,8,32,512]{3,2,1,0:T(8,128)(2,1)S(1)} async-done(((bf16[4,8,32,512]{3,2,1,0:T(8,128)(2,1)}), bf16[4,8,32,512]{3,2,1,0:T(8,128)(2,1)S(1)}, u32[]{:S(2)}, u32[]{:S(2)}) %all-to-all-start.2) | async-done | bytes 1048608 | tf_op jit(solution)/shard_map/all_to_all | solution.py:131
  505.7 5.0 all-to-all-start.3
  513.5 11.7 %all-to-all-done.3 = bf16[8,32,2048]{2,1,0:T(8,128)(2,1)S(1)} async-done(((bf16[8,32,2048]{2,1,0:T(8,128)(2,1)}), bf16[8,32,2048]{2,1,0:T(8,128)(2,1)S(1)}, u32[]{:S(2)}, u32[]{:S(2)}) %all-to-all-start.3) | async-done | bytes 1048608 | tf_op jit(solution)/shard_map/all_to_all | solution.py:139
  526.9 8.4 %gather_fusion.1 = bf16[512,2048]{1,0:T(8,128)(2,1)S(1)} fusion(bf16[8,32,2048]{2,1,0:T(8,128)(2,1)S(1)} %reshape.184, s32[512]{0:T(512)S(1)} %reshape.195), kind=kCustom, calls=%fused_computation.1 | custom fusion | bytes 4198400 | tf_op jit(solution)/shard_map/vmap(jit(_take))/gather | solution.py:151
  538.4 5.1 all-to-all-start.4
  546.3 11.4 %all-to-all-done.4 = f32[4,2,8,2048]{3,2,1,0:T(8,128)} async-done(((f32[4,2,8,2048]{3,2,1,0:T(8,128)}), f32[4,2,8,2048]{3,2,1,0:T(8,128)}, u32[]{:S(2)}, u32[]{:S(2)}) %all-to-all-start.4) | async-done | bytes 524320 | tf_op jit(solution)/shard_map/all_to_all | solution.py:156
  558.9 5.4 collective-permute-start.4
  (79 shorter events, 52.0 us)
Async XLA Ops:
  7.2 176.8 %all-gather.5.cloned.1.call-start = ((), (), s32[]{:S(2)}) async-start(), calls=%async_computation.5 | async-start | bytes 10485760 | tf_op jit(solution)/shard_map/all_gather | solution.py:116
  7.2 9.1 %collective-permute-start = (s32[8,8]{1,0:T(8,128)}, s32[8,8]{1,0:T(8,128)S(1)}, u32[]{:S(2)}, u32[]{:S(2)}) collective-permute-start(s32[8,8]{1,0:T(8,128)} %param.10), channel_id=1, source_target_pairs={{0,4},{1,5},{2,6},{3,7},{4,0},{5,1},{6,2},{7,3},{8,12},{9,13},{10,... | collective-permute-start | bytes 776 | tf_op jit(solution)/shard_map/ppermute | solution.py:93
  14.5 21.2 %collective-permute-start.2 = (bf16[8,4096]{1,0:T(8,128)(2,1)}, bf16[8,4096]{1,0:T(8,128)(2,1)S(1)}, u32[]{:S(2)}, u32[]{:S(2)}) collective-permute-start(bf16[8,4096]{1,0:T(8,128)(2,1)} %param.9), channel_id=1, source_target_pairs={{0,4},{1,5},{2,6},{3,7},{4,0},{5,1},{6,2},{7,3},{8,12},{9,13},{10,... | collective-permute-start | bytes 196616 | tf_op jit(solution)/shard_map/ppermute | solution.py:92
  98.2 373.7 %all-gather.7.cloned.1.call-start = ((), (), s32[]{:S(2)}) async-start(), calls=%async_computation.6 | async-start | bytes 3932160 | tf_op jit(solution)/shard_map/all_gather | solution.py:121
  183.9 6.9 %copy-start.3 = (bf16[32,32,4096]{2,1,0:T(8,128)(2,1)S(1)}, bf16[32,32,4096]{2,1,0:T(8,128)(2,1)}, u32[]{:S(2)}) copy-start(bf16[32,32,4096]{2,1,0:T(8,128)(2,1)} %all-gather.5.cloned.1.call-done) | copy-start | bytes 25165828
  195.2 18.5 %collective-permute-start.3 = (bf16[1024,192]{0,1:T(8,128)(2,1)S(1)}, bf16[1024,192]{0,1:T(8,128)(2,1)S(1)}, u32[]{:S(2)}, u32[]{:S(2)}) collective-permute-start(bf16[1024,192]{0,1:T(8,128)(2,1)S(1)} %fusion.10), channel_id=1, source_target_pairs={{0,4},{1,5},{2,6},{3,7},{4,0},{5,1},{6,2},{7,3},{8,12},{9,13},{10,... | collective-permute-start | bytes 1179656 | tf_op jit(solution)/shard_map/ppermute | solution.py:120
  218.4 17.4 %copy-start.1 = (f32[8,8]{1,0:T(8,128)S(1)}, f32[8,8]{1,0:T(8,128)}, u32[]{:S(2)}) copy-start(f32[8,8]{1,0:T(8,128)} %param.11) | copy-start | bytes 772
  218.4 23.3 %copy-start.2 = (s32[8,2]{0,1:T(2,128)S(1)}, s32[8,2]{0,1:T(2,128)}, u32[]{:S(2)}) copy-start(s32[8,2]{0,1:T(2,128)} %param.13) | copy-start | bytes 196
  218.4 261.6 %all-to-all-start.1 = ((bf16[192,8,512]{2,0,1:T(8,128)(2,1)}), bf16[192,8,512]{2,0,1:T(8,128)(2,1)}, u32[]{:S(2)}, u32[]{:S(2)}) async-start(bf16[192,8,512]{2,0,1:T(8,128)(2,1)} %copy.97), calls=%async_computation.1 | async-start | bytes 3145728 | tf_op jit(solution)/shard_map/all_to_all | solution.py:85
  232.4 257.5 %collective-permute-start.5 = (bf16[1,192,4096]{2,1,0:T(8,128)(2,1)}, bf16[1,192,4096]{2,1,0:T(8,128)(2,1)}, u32[]{:S(2)}, u32[]{:S(2)}) collective-permute-start(bf16[1,192,4096]{2,1,0:T(8,128)(2,1)} %param.15), channel_id=1, source_target_pairs={{0,128},{8,136},{16,144},{24,152},{32,160},{40,168},{48,176},{56,1... | collective-permute-start | bytes 4718600 | tf_op jit(solution)/shard_map/ppermute | solution.py:84
  232.9 277.9 %collective-permute-start.6 = (bf16[1,192,4096]{2,1,0:T(8,128)(2,1)}, bf16[1,192,4096]{2,1,0:T(8,128)(2,1)}, u32[]{:S(2)}, u32[]{:S(2)}) collective-permute-start(bf16[1,192,4096]{2,1,0:T(8,128)(2,1)} %param.16), channel_id=1, source_target_pairs={{0,128},{8,136},{16,144},{24,152},{32,160},{40,168},{48,176},{56,1... | collective-permute-start | bytes 4718600 | tf_op jit(solution)/shard_map/ppermute | solution.py:84
  235.3 308.2 %collective-permute-start.7 = (bf16[1,192,4096]{2,1,0:T(8,128)(2,1)}, bf16[1,192,4096]{2,1,0:T(8,128)(2,1)}, u32[]{:S(2)}, u32[]{:S(2)}) collective-permute-start(bf16[1,192,4096]{2,1,0:T(8,128)(2,1)} %param.17), channel_id=1, source_target_pairs={{0,128},{8,136},{16,144},{24,152},{32,160},{40,168},{48,176},{56,1... | collective-permute-start | bytes 4718600 | tf_op jit(solution)/shard_map/ppermute | solution.py:84
  235.8 132.2 %collective-permute-start.1 = (f32[8,8]{1,0:T(8,128)S(1)}, f32[8,8]{1,0:T(8,128)S(1)}, u32[]{:S(2)}, u32[]{:S(2)}) collective-permute-start(f32[8,8]{1,0:T(8,128)S(1)} %copy-done.1), channel_id=1, source_target_pairs={{0,4},{1,5},{2,6},{3,7},{4,0},{5,1},{6,2},{7,3},{8,12},{9,13},{10,... | collective-permute-start | bytes 776 | tf_op jit(solution)/shard_map/ppermute | solution.py:94
  485.3 18.0 %all-to-all-start.2 = ((bf16[4,8,32,512]{3,2,1,0:T(8,128)(2,1)}), bf16[4,8,32,512]{3,2,1,0:T(8,128)(2,1)S(1)}, u32[]{:S(2)}, u32[]{:S(2)}) async-start(bf16[4,8,32,512]{3,2,1,0:T(8,128)(2,1)} %bitcast.23), calls=%async_computation.2 | async-start | bytes 2097152 | tf_op jit(solution)/shard_map/all_to_all | solution.py:131
  505.7 19.5 %all-to-all-start.3 = ((bf16[8,32,2048]{2,1,0:T(8,128)(2,1)}), bf16[8,32,2048]{2,1,0:T(8,128)(2,1)S(1)}, u32[]{:S(2)}, u32[]{:S(2)}) async-start(bf16[8,32,2048]{2,1,0:T(8,128)(2,1)} %reshape.182), calls=%async_computation.3 | async-start | bytes 2097152 | tf_op jit(solution)/shard_map/all_to_all | solution.py:139
  538.4 19.4 %all-to-all-start.4 = ((f32[4,2,8,2048]{3,2,1,0:T(8,128)}), f32[4,2,8,2048]{3,2,1,0:T(8,128)}, u32[]{:S(2)}, u32[]{:S(2)}) async-start(f32[4,2,8,2048]{3,2,1,0:T(8,128)} %bitcast.30), calls=%async_computation.4 | async-start | bytes 1048576 | tf_op jit(solution)/shard_map/all_to_all | solution.py:156
  543.5 20.8 %copy-start = (bf16[2,4096,192]{1,2,0:T(8,128)(2,1)S(1)}, bf16[2,4096,192]{1,2,0:T(8,128)(2,1)}, u32[]{:S(2)}) copy-start(bf16[2,4096,192]{1,2,0:T(8,128)(2,1)} %all-gather.7.cloned.1.call-done) | copy-start | bytes 9437188
  558.9 13.0 %collective-permute-start.4 = (bf16[8,2048]{1,0:T(8,128)(2,1)S(1)}, bf16[8,2048]{1,0:T(8,128)(2,1)S(1)}, u32[]{:S(2)}, u32[]{:S(2)}) collective-permute-start(bf16[8,2048]{1,0:T(8,128)(2,1)S(1)} %get-tuple-element.15), channel_id=1, source_target_pairs={{0,4},{1,5},{2,6},{3,7},{4,0},{5,1},{6,2},{7,3},{8,12},{9,13},{10,... | collective-permute-start | bytes 98312 | tf_op jit(solution)/shard_map/ppermute | solution.py:167
  566.0 4.5 collective-permute-start.8
Sparse Core Ops, SparseCore 0:
  98.3 85.5 all-gather.4
  214.9 60.3 all-gather.6

commit v5 on v3

--- a/solution.py
+++ b/solution.py
@@ -92,6 +92,7 @@
     picked = jax.vmap(lambda t, s: jnp.take(t, s, axis=0))(blk_tokens, source)
     outgoing = jnp.where(filled[..., None], picked, jnp.zeros((), jnp.bfloat16))
     outgoing = outgoing.reshape(HALVES, experts, CAP, width).transpose(1, 0, 2, 3)
+    outgoing = outgoing.reshape(experts, HALVES * CAP, width)
     arrived_rows = lax.all_to_all(outgoing, "expert", 0, 0, tiled=True)
     group_rows = lax.all_gather(
         arrived_rows, "replica", axis=0, tiled=False, axis_index_groups=ygroups
@@ -99,26 +100,27 @@
     hidden = expert_hidden(group_rows, w_gate[0], w_up[0]).reshape(-1, units)
     pair_hidden = canonical(hidden, lax.ppermute(hidden, "replica", across), first)
     hidden_all = lax.all_gather(
-        pair_hidden, "replica", axis=1, tiled=False, axis_index_groups=ygroups
-    ).reshape(replicas, -1, units)
+        pair_hidden, "replica", axis=0, tiled=False, axis_index_groups=ygroups
+    )
     group_peak = jnp.max(jnp.abs(hidden_all)).astype(jnp.float32)
+    expert_peak = jnp.where(swapped, lax.ppermute(group_peak, "expert", ring), group_peak)
     out_cols = lax.dot_general(
         hidden_all,
-        down_cols,
-        (((0, 2), (0, 1)), ((), ())),
+        down_cols.reshape(HALVES, ys, units, cols),
+        (((0, 1, 3), (1, 0, 2)), ((), ())),
         preferred_element_type=jnp.float32,
     ).astype(jnp.bfloat16)
     half_rows = lax.all_to_all(
-        out_cols.reshape(ys, experts, HALVES, CAP, cols),
+        out_cols.reshape(ys, experts, HALVES * CAP, cols),
         "replica",
         split_axis=0,
-        concat_axis=4,
+        concat_axis=3,
         tiled=True,
         axis_index_groups=ygroups,
     )
     returned = lax.all_to_all(
-        half_rows.reshape(experts, HALVES, CAP, ys * cols), "expert", 0, 0, tiled=True
-    )
+        half_rows.reshape(experts, HALVES * CAP, ys * cols), "expert", 0, 0, tiled=True
+    ).reshape(experts, HALVES, CAP, ys * cols)
     by_block = returned.transpose(1, 0, 2, 3).reshape(HALVES, experts * CAP, ys * cols)
     fetched = jax.vmap(lambda t, s: jnp.take(t, s, axis=0))(by_block, slot_of)
     scales = jnp.where(slot_kept, blk_gw.reshape(HALVES, -1), jnp.float32(0.0))
@@ -136,7 +138,6 @@
     moved_gate, moved_up, moved_down = (
         jnp.where(swapped, got, own) for got, own in zip(arrived, (w_gate, w_up, w_down))
     )
-    expert_peak = jnp.where(swapped, lax.ppermute(group_peak, "expert", ring), group_peak)
     return (moe_output, moved_gate, moved_up, moved_down, expert_peak.reshape(1))
 
 

time: 524 us -> 514 us (0.981)
  local copies, waits for them, and re-layouts: 42.1 us -> 23.5 us
  waiting for transfers between devices: 317 us -> 325 us
    all_to_all x1, waiting for transfers between devices: 0.01 us -> 32 us  [shards(): lax.all_to_all(w_down[0].reshape(units, replicas, cols), 'replica', split...]
    all_gather x1, waiting for transfers between devices: 33.4 us -> 1.83 us  [shards(): lax.all_gather(pair_hidden, 'replica', axis=0, tiled=False, axis_index_gr...]
    reshape x6 -> x2, local copies, waits for them, and re-layouts: 19.4 us -> 3.78 us  [the longest x1 2.63 us: shards(): half_rows.reshape(experts, HALVES * CAP, ys * cols)]
    ppermute x1, waiting for transfers between devices: 74 us -> 82.9 us  [shards(): lax.ppermute(gate_weights, 'replica', across)]
  transfers between devices with their start and end apart: 14 -> 14, of which waited for: 10 -> 11; matrix products, arithmetic and copies ran while one was open for 7% -> 5% of each run, Pallas kernels for 0% -> 0%
where the time goes in v5:
time: 514 us; the launch traced here: 513 us
  waiting for transfers between devices  325 us (63%)
  starting transfers between devices  56.1 us (11%)
  blocking collectives  54.6 us (11%)
  local copies, waits for them, and re-layouts  23.5 us (5%)
  other arithmetic  20 us (4%)
  between operations  18 us (4%)
  matrix products  15.9 us (3%)
    ppermute x3, waiting for transfers between devices, shards(): lax.ppermute(w, 'expert', ring)  93.8 us
    all_gather x1, waiting for transfers between devices, shards(): lax.all_gather(arrived_rows, 'replica', axis=0, tiled=False, axis_index_g...  82.9 us
    ppermute x1, waiting for transfers between devices, shards(): lax.ppermute(gate_weights, 'replica', across)  82.9 us
    all_to_all x1, blocking collectives, shards(): arrived_rows = lax.all_to_all(outgoing, 'expert', 0, 0, tiled=True)  54.6 us
    all_to_all x1, waiting for transfers between devices, shards(): lax.all_to_all(w_down[0].reshape(units, replicas, cols), 'replica', split...  32 us
    all_to_all x1, starting transfers between devices, shards(): lax.all_to_all(w_down[0].reshape(units, replicas, cols), 'replica', split...  13.9 us
    ppermute x1, waiting for transfers between devices, shards(): lax.ppermute(hidden, 'replica', across)  12.7 us
  transfers between devices with their start and end apart: 14, of which 11 were waited for; matrix products, arithmetic and copies ran while one was open for 5% of the time, Pallas kernels for 0%

profile of v5, /device:TPU:2, one launch (start us, length us, event | category | flops | bytes accessed | tf_op | source)
XLA Modules:
  0.0 513.3 jit_solution(8166486678169143870)
XLA Ops:
  7.2 7.3 %collective-permute-start.2 = (bf16[8,4096]{1,0:T(8,128)(2,1)}, bf16[8,4096]{1,0:T(8,128)(2,1)S(1)}, u32[]{:S(2)}, u32[]{:S(2)}) collective-permute-start(bf16[8,4096]{1,0:T(8,128)(2,1)} %param.9), channel_id=1, source_target_pairs={{0,4},{1,5},{2,6},{3,7},{4,0},{5,1},{6,2},{7,3},{8,12},{9,13},{10,... | collective-permute-start | bytes 196616 | tf_op jit(solution)/shard_map/ppermute | solution.py:86
  14.6 7.7 %collective-permute-done = s32[8,8]{1,0:T(8,128)S(1)} collective-permute-done((s32[8,8]{1,0:T(8,128)}, s32[8,8]{1,0:T(8,128)S(1)}, u32[]{:S(2)}, u32[]{:S(2)}) %collective-permute-start) | collective-permute-done | bytes 288 | tf_op jit(solution)/shard_map/ppermute | solution.py:87
  25.8 7.2 %gather_fusion = bf16[256,4096]{1,0:T(8,128)(2,1)S(1)} fusion(bf16[2,8,4096]{2,1,0:T(8,128)(2,1)S(1)} %pad_maximum_fusion.1, s32[256]{0:T(256)S(1)} %fusion.24), kind=kCustom, calls=%fused_computation | custom fusion | bytes 4196352 | tf_op jit(solution)/shard_map/vmap(jit(_take))/gather | solution.py:92
  35.2 4.2 fusion.4
  40.6 54.6 %all_to_all.40 = bf16[32,8,4096]{2,1,0:T(8,128)(2,1)} all-to-all(bf16[32,8,4096]{2,1,0:T(8,128)(2,1)S(1)} %copy.51), channel_id=1, replica_groups=mesh['expert'=32,'replica'=8] {'expert'}, dimensions={0} | all-to-all | bytes 4194304 | tf_op jit(solution)/shard_map/all_to_all | solution.py:96
  95.2 82.9 %all-gather.5.cloned.1.call-done = bf16[128,8,4096]{2,1,0:T(8,128)(2,1)} async-done(((bf16[32,8,4096]{2,1,0:T(8,128)(2,1)}), bf16[128,8,4096]{2,1,0:T(8,128)(2,1)}) %all-gather.5.cloned.1.call-update) | async-done | bytes 8388624 | tf_op jit(solution)/shard_map/all_gather | solution.py:97
  178.2 6.8 %fusion.2 = f32[1024,192]{0,1:T(8,128)S(1)} fusion(bf16[128,8,4096]{2,1,0:T(8,128)(2,1)} %all-gather.5.cloned.1.call-done, bf16[1,192,4096]{2,1,0:T(8,128)(2,1)} %param.15), kind=kOutput, calls=%fused_computation.4 | convolution fusion | flops 1610612736 | bytes 10747904 | tf_op jit(solution)/shard_map/dot_general | solution.py:47
  185.0 4.4 fusion.13
  189.4 5.8 %collective-permute-start.3 = (bf16[1024,192]{0,1:T(8,128)(2,1)S(1)}, bf16[1024,192]{0,1:T(8,128)(2,1)S(1)}, u32[]{:S(2)}, u32[]{:S(2)}) collective-permute-start(bf16[1024,192]{0,1:T(8,128)(2,1)S(1)} %fusion.13), channel_id=1, source_target_pairs={{0,4},{1,5},{2,6},{3,7},{4,0},{5,1},{6,2},{7,3},{8,12},{9,13},{10,... | collective-permute-start | bytes 1179656 | tf_op jit(solution)/shard_map/ppermute | solution.py:101
  195.2 12.7 %collective-permute-done.3 = bf16[1024,192]{0,1:T(8,128)(2,1)S(1)} collective-permute-done((bf16[1024,192]{0,1:T(8,128)(2,1)S(1)}, bf16[1024,192]{0,1:T(8,128)(2,1)S(1)}, u32[]{:S(2)}, u32[]{:S(2)}) %collective-permute-start.3) | collective-permute-done | bytes 393248 | tf_op jit(solution)/shard_map/ppermute | solution.py:101
  212.0 13.9 %all-to-all-start.1 = ((bf16[192,8,512]{2,0,1:T(8,128)(2,1)}), bf16[192,8,512]{2,0,1:T(8,128)(2,1)S(1)}, u32[]{:S(2)}, u32[]{:S(2)}) async-start(bf16[192,8,512]{2,0,1:T(8,128)(2,1)} %copy.52), calls=%async_computation.1 | async-start | bytes 3145728 | tf_op jit(solution)/shard_map/all_to_all | solution.py:79
  229.3 5.9 %collective-permute-start.1 = (f32[8,8]{1,0:T(8,128)S(1)}, f32[8,8]{1,0:T(8,128)S(1)}, u32[]{:S(2)}, u32[]{:S(2)}) collective-permute-start(f32[8,8]{1,0:T(8,128)S(1)} %copy-done.1), channel_id=1, source_target_pairs={{0,4},{1,5},{2,6},{3,7},{4,0},{5,1},{6,2},{7,3},{8,12},{9,13},{10,... | collective-permute-start | bytes 776 | tf_op jit(solution)/shard_map/ppermute | solution.py:88
  235.4 32.0 %all-to-all-done.1 = bf16[192,8,512]{2,0,1:T(8,128)(2,1)S(1)} async-done(((bf16[192,8,512]{2,0,1:T(8,128)(2,1)}), bf16[192,8,512]{2,0,1:T(8,128)(2,1)S(1)}, u32[]{:S(2)}, u32[]{:S(2)}) %all-to-all-start.1) | async-done | bytes 1572896 | tf_op jit(solution)/shard_map/all_to_all | solution.py:79
  269.1 4.7 bitcast_convert_fusion
  273.8 3.5 all-to-all-start.2
  278.6 82.9 %collective-permute-done.1 = f32[8,8]{1,0:T(8,128)S(1)} collective-permute-done((f32[8,8]{1,0:T(8,128)S(1)}, f32[8,8]{1,0:T(8,128)S(1)}, u32[]{:S(2)}, u32[]{:S(2)}) %collective-permute-start.1) | collective-permute-done | bytes 288 | tf_op jit(solution)/shard_map/ppermute | solution.py:88
  366.2 8.9 %all-to-all-start.3 = ((bf16[32,8,2048]{2,1,0:T(8,128)(2,1)}), bf16[32,8,2048]{2,1,0:T(8,128)(2,1)S(1)}, u32[]{:S(2)}, u32[]{:S(2)}) async-start(bf16[32,8,2048]{2,1,0:T(8,128)(2,1)} %reshape.164), calls=%async_computation.3 | async-start | bytes 2097152 | tf_op jit(solution)/shard_map/all_to_all | solution.py:121
  375.2 30.4 %collective-permute-done.7 = bf16[1,192,4096]{2,1,0:T(8,128)(2,1)} collective-permute-done((bf16[1,192,4096]{2,1,0:T(8,128)(2,1)S(1)}, bf16[1,192,4096]{2,1,0:T(8,128)(2,1)}, u32[]{:S(2)}, u32[]{:S(2)}) %collective-permute-start.7) | collective-permute-done | bytes 1572896 | tf_op jit(solution)/shard_map/ppermute | solution.py:78
  406.9 32.4 %collective-permute-done.6 = bf16[1,192,4096]{2,1,0:T(8,128)(2,1)} collective-permute-done((bf16[1,192,4096]{2,1,0:T(8,128)(2,1)}, bf16[1,192,4096]{2,1,0:T(8,128)(2,1)}, u32[]{:S(2)}, u32[]{:S(2)}) %collective-permute-start.6) | collective-permute-done | bytes 1572896 | tf_op jit(solution)/shard_map/ppermute | solution.py:78
  442.0 31.0 %collective-permute-done.5 = bf16[1,192,4096]{2,1,0:T(8,128)(2,1)} collective-permute-done((bf16[1,192,4096]{2,1,0:T(8,128)(2,1)}, bf16[1,192,4096]{2,1,0:T(8,128)(2,1)}, u32[]{:S(2)}, u32[]{:S(2)}) %collective-permute-start.5) | collective-permute-done | bytes 1572896 | tf_op jit(solution)/shard_map/ppermute | solution.py:78
  475.7 8.3 %all-to-all-done.3 = bf16[32,8,2048]{2,1,0:T(8,128)(2,1)S(1)} async-done(((bf16[32,8,2048]{2,1,0:T(8,128)(2,1)}), bf16[32,8,2048]{2,1,0:T(8,128)(2,1)S(1)}, u32[]{:S(2)}, u32[]{:S(2)}) %all-to-all-start.3) | async-done | bytes 1048608 | tf_op jit(solution)/shard_map/all_to_all | solution.py:121
  489.3 5.7 %collective-permute-start.4 = (bf16[8,2048]{1,0:T(8,128)(2,1)S(1)}, bf16[8,2048]{1,0:T(8,128)(2,1)S(1)}, u32[]{:S(2)}, u32[]{:S(2)}) collective-permute-start(bf16[8,2048]{1,0:T(8,128)(2,1)S(1)} %get-tuple-element.17), channel_id=1, source_target_pairs={{0,4},{1,5},{2,6},{3,7},{4,0},{5,1},{6,2},{7,3},{8,12},{9,13},{10,... | collective-permute-start | bytes 98312 | tf_op jit(solution)/shard_map/ppermute | solution.py:132
  495.0 3.2 abs_reduce_fusion
  500.2 3.1 collective-permute-done.8
  (68 shorter events, 35.8 us)
Async XLA Ops:
  7.2 171.0 %all-gather.5.cloned.1.call-start = ((), (), s32[]{:S(2)}) async-start(), calls=%async_computation.4 | async-start | bytes 10485760 | tf_op jit(solution)/shard_map/all_gather | solution.py:97
  7.2 17.7 %collective-permute-start.2 = (bf16[8,4096]{1,0:T(8,128)(2,1)}, bf16[8,4096]{1,0:T(8,128)(2,1)S(1)}, u32[]{:S(2)}, u32[]{:S(2)}) collective-permute-start(bf16[8,4096]{1,0:T(8,128)(2,1)} %param.9), channel_id=1, source_target_pairs={{0,4},{1,5},{2,6},{3,7},{4,0},{5,1},{6,2},{7,3},{8,12},{9,13},{10,... | collective-permute-start | bytes 196616 | tf_op jit(solution)/shard_map/ppermute | solution.py:86
  14.5 7.8 %collective-permute-start = (s32[8,8]{1,0:T(8,128)}, s32[8,8]{1,0:T(8,128)S(1)}, u32[]{:S(2)}, u32[]{:S(2)}) collective-permute-start(s32[8,8]{1,0:T(8,128)} %param.10), channel_id=1, source_target_pairs={{0,4},{1,5},{2,6},{3,7},{4,0},{5,1},{6,2},{7,3},{8,12},{9,13},{10,... | collective-permute-start | bytes 776 | tf_op jit(solution)/shard_map/ppermute | solution.py:87
  95.2 174.0 %all-gather.7.cloned.1.call-start = ((), (), s32[]{:S(2)}) async-start(), calls=%async_computation.5 | async-start | bytes 3932160 | tf_op jit(solution)/shard_map/all_gather | solution.py:102
  178.2 6.9 %copy-start.3 = (bf16[128,8,4096]{2,1,0:T(8,128)(2,1)S(1)}, bf16[128,8,4096]{2,1,0:T(8,128)(2,1)}, u32[]{:S(2)}) copy-start(bf16[128,8,4096]{2,1,0:T(8,128)(2,1)} %all-gather.5.cloned.1.call-done) | copy-start | bytes 25165828
  189.4 18.5 %collective-permute-start.3 = (bf16[1024,192]{0,1:T(8,128)(2,1)S(1)}, bf16[1024,192]{0,1:T(8,128)(2,1)S(1)}, u32[]{:S(2)}, u32[]{:S(2)}) collective-permute-start(bf16[1024,192]{0,1:T(8,128)(2,1)S(1)} %fusion.13), channel_id=1, source_target_pairs={{0,4},{1,5},{2,6},{3,7},{4,0},{5,1},{6,2},{7,3},{8,12},{9,13},{10,... | collective-permute-start | bytes 1179656 | tf_op jit(solution)/shard_map/ppermute | solution.py:101
  208.0 1.7 copy-start
  212.0 17.4 %copy-start.1 = (f32[8,8]{1,0:T(8,128)S(1)}, f32[8,8]{1,0:T(8,128)}, u32[]{:S(2)}) copy-start(f32[8,8]{1,0:T(8,128)} %param.11) | copy-start | bytes 772
  212.0 23.3 %copy-start.2 = (s32[8,2]{0,1:T(2,128)S(1)}, s32[8,2]{0,1:T(2,128)}, u32[]{:S(2)}) copy-start(s32[8,2]{0,1:T(2,128)} %param.13) | copy-start | bytes 196
  212.0 55.4 %all-to-all-start.1 = ((bf16[192,8,512]{2,0,1:T(8,128)(2,1)}), bf16[192,8,512]{2,0,1:T(8,128)(2,1)S(1)}, u32[]{:S(2)}, u32[]{:S(2)}) async-start(bf16[192,8,512]{2,0,1:T(8,128)(2,1)} %copy.52), calls=%async_computation.1 | async-start | bytes 3145728 | tf_op jit(solution)/shard_map/all_to_all | solution.py:79
  225.9 179.7 %collective-permute-start.7 = (bf16[1,192,4096]{2,1,0:T(8,128)(2,1)S(1)}, bf16[1,192,4096]{2,1,0:T(8,128)(2,1)}, u32[]{:S(2)}, u32[]{:S(2)}) collective-permute-start(bf16[1,192,4096]{2,1,0:T(8,128)(2,1)S(1)} %copy-done), channel_id=1, source_target_pairs={{0,128},{8,136},{16,144},{24,152},{32,160},{40,168},{48,176},{56,1... | collective-permute-start | bytes 4718600 | tf_op jit(solution)/shard_map/ppermute | solution.py:78
  226.4 212.8 %collective-permute-start.6 = (bf16[1,192,4096]{2,1,0:T(8,128)(2,1)}, bf16[1,192,4096]{2,1,0:T(8,128)(2,1)}, u32[]{:S(2)}, u32[]{:S(2)}) collective-permute-start(bf16[1,192,4096]{2,1,0:T(8,128)(2,1)} %param.16), channel_id=1, source_target_pairs={{0,128},{8,136},{16,144},{24,152},{32,160},{40,168},{48,176},{56,1... | collective-permute-start | bytes 4718600 | tf_op jit(solution)/shard_map/ppermute | solution.py:78
  228.8 244.1 %collective-permute-start.5 = (bf16[1,192,4096]{2,1,0:T(8,128)(2,1)}, bf16[1,192,4096]{2,1,0:T(8,128)(2,1)}, u32[]{:S(2)}, u32[]{:S(2)}) collective-permute-start(bf16[1,192,4096]{2,1,0:T(8,128)(2,1)} %param.15), channel_id=1, source_target_pairs={{0,128},{8,136},{16,144},{24,152},{32,160},{40,168},{48,176},{56,1... | collective-permute-start | bytes 4718600 | tf_op jit(solution)/shard_map/ppermute | solution.py:78
  229.3 132.2 %collective-permute-start.1 = (f32[8,8]{1,0:T(8,128)S(1)}, f32[8,8]{1,0:T(8,128)S(1)}, u32[]{:S(2)}, u32[]{:S(2)}) collective-permute-start(f32[8,8]{1,0:T(8,128)S(1)} %copy-done.1), channel_id=1, source_target_pairs={{0,4},{1,5},{2,6},{3,7},{4,0},{5,1},{6,2},{7,3},{8,12},{9,13},{10,... | collective-permute-start | bytes 776 | tf_op jit(solution)/shard_map/ppermute | solution.py:88
  273.8 88.0 %all-to-all-start.2 = ((bf16[4,32,8,512]{3,2,1,0:T(8,128)(2,1)}), bf16[4,32,8,512]{3,2,1,0:T(8,128)(2,1)S(1)}, u32[]{:S(2)}, u32[]{:S(2)}) async-start(bf16[4,32,8,512]{3,2,1,0:T(8,128)(2,1)} %bitcast.90), calls=%async_computation.2 | async-start | bytes 2097152 | tf_op jit(solution)/shard_map/all_to_all | solution.py:113
  366.2 117.8 %all-to-all-start.3 = ((bf16[32,8,2048]{2,1,0:T(8,128)(2,1)}), bf16[32,8,2048]{2,1,0:T(8,128)(2,1)S(1)}, u32[]{:S(2)}, u32[]{:S(2)}) async-start(bf16[32,8,2048]{2,1,0:T(8,128)(2,1)} %reshape.164), calls=%async_computation.3 | async-start | bytes 2097152 | tf_op jit(solution)/shard_map/all_to_all | solution.py:121
  489.3 15.4 %collective-permute-start.4 = (bf16[8,2048]{1,0:T(8,128)(2,1)S(1)}, bf16[8,2048]{1,0:T(8,128)(2,1)S(1)}, u32[]{:S(2)}, u32[]{:S(2)}) collective-permute-start(bf16[8,2048]{1,0:T(8,128)(2,1)S(1)} %get-tuple-element.17), channel_id=1, source_target_pairs={{0,4},{1,5},{2,6},{3,7},{4,0},{5,1},{6,2},{7,3},{8,12},{9,13},{10,... | collective-permute-start | bytes 98312 | tf_op jit(solution)/shard_map/ppermute | solution.py:132
  498.8 4.5 collective-permute-start.8
Sparse Core Ops, SparseCore 0:
  95.3 82.8 all-gather.4
  209.1 60.0 all-gather.6

commit v6 on v5

--- a/solution.py
+++ b/solution.py
@@ -83,9 +83,17 @@
         concat_axis=0,
         tiled=True,
     ).reshape(replicas, units, cols)
-    blk_tokens = canonical(tokens, lax.ppermute(tokens, "replica", across), first)
-    blk_ids = canonical(expert_ids, lax.ppermute(expert_ids, "replica", across), first)
-    blk_gw = canonical(gate_weights, lax.ppermute(gate_weights, "replica", across), first)
+    gw_hi = gate_weights.astype(jnp.bfloat16)
+    gw_lo = (gate_weights - gw_hi.astype(jnp.float32)).astype(jnp.bfloat16)
+    packed = jnp.concatenate([tokens, expert_ids.astype(jnp.bfloat16), gw_hi, gw_lo], axis=1)
+    got = lax.ppermute(packed, "replica", across)
+    their_ids = got[:, width : width + TOPK].astype(jnp.int32)
+    their_gw = got[:, width + TOPK : width + 2 * TOPK].astype(jnp.float32) + got[
+        :, width + 2 * TOPK :
+    ].astype(jnp.float32)
+    blk_tokens = canonical(tokens, got[:, :width], first)
+    blk_ids = canonical(expert_ids, their_ids, first)
+    blk_gw = canonical(gate_weights, their_gw, first)
     slot_of, slot_kept, source, filled = jax.vmap(route_slots, in_axes=(0, None, None))(
         blk_ids, expert_holder, capacity
     )
@@ -103,7 +111,6 @@
         pair_hidden, "replica", axis=0, tiled=False, axis_index_groups=ygroups
     )
     group_peak = jnp.max(jnp.abs(hidden_all)).astype(jnp.float32)
-    expert_peak = jnp.where(swapped, lax.ppermute(group_peak, "expert", ring), group_peak)
     out_cols = lax.dot_general(
         hidden_all,
         down_cols.reshape(HALVES, ys, units, cols),
@@ -138,6 +145,7 @@
     moved_gate, moved_up, moved_down = (
         jnp.where(swapped, got, own) for got, own in zip(arrived, (w_gate, w_up, w_down))
     )
+    expert_peak = jnp.where(swapped, lax.ppermute(group_peak, "expert", ring), group_peak)
     return (moe_output, moved_gate, moved_up, moved_down, expert_peak.reshape(1))
 
 

time: 514 us -> 516 us (level)
  starting transfers between devices: 56.1 us -> 48.4 us
  waiting for transfers between devices: 325 us -> 331 us
    ppermute x3 -> x1, waiting for transfers between devices: 90.6 us -> 2.52 us  [shards(): got = lax.ppermute(packed, 'replica', across)]
    ppermute x3, waiting for transfers between devices: 93.8 us -> 163 us  [shards(): lax.ppermute(w, 'expert', ring)]
    all_to_all x1, waiting for transfers between devices: 0.01 us -> 13.9 us  [shards(): lax.all_to_all(out_cols.reshape(ys, experts, HALVES * CAP, cols), 'replic...]
    ppermute x3 -> x1, starting transfers between devices: 13.3 us -> 7.2 us  [shards(): got = lax.ppermute(packed, 'replica', across)]
    all_to_all x1, waiting for transfers between devices: 32 us -> 37.8 us  [shards(): lax.all_to_all(w_down[0].reshape(units, replicas, cols), 'replica', split...]
  transfers between devices with their start and end apart: 14 -> 12, of which waited for: 11 -> 11; matrix products, arithmetic and copies ran while one was open for 5% -> 4% of each run, Pallas kernels for 0% -> 0%
where the time goes in v6:
time: 516 us; the launch traced here: 515 us
  waiting for transfers between devices  331 us (64%)
  blocking collectives  55.8 us (11%)
  starting transfers between devices  48.4 us (9%)
  local copies, waits for them, and re-layouts  24.4 us (5%)
  other arithmetic  21.5 us (4%)
  between operations  17.9 us (3%)
  matrix products  15.9 us (3%)
    ppermute x3, waiting for transfers between devices, shards(): lax.ppermute(w, 'expert', ring)  163 us
    all_gather x1, waiting for transfers between devices, shards(): lax.all_gather(arrived_rows, 'replica', axis=0, tiled=False, axis_index_g...  86.5 us
    all_to_all x1, blocking collectives, shards(): arrived_rows = lax.all_to_all(outgoing, 'expert', 0, 0, tiled=True)  55.8 us
    all_to_all x1, waiting for transfers between devices, shards(): lax.all_to_all(w_down[0].reshape(units, replicas, cols), 'replica', split...  37.8 us
    all_to_all x1, starting transfers between devices, shards(): lax.all_to_all(w_down[0].reshape(units, replicas, cols), 'replica', split...  13.9 us
    all_to_all x1, waiting for transfers between devices, shards(): lax.all_to_all(out_cols.reshape(ys, experts, HALVES * CAP, cols), 'replic...  13.9 us
    ppermute x1, waiting for transfers between devices, shards(): lax.ppermute(hidden, 'replica', across)  12.7 us
  transfers between devices with their start and end apart: 12, of which 11 were waited for; matrix products, arithmetic and copies ran while one was open for 4% of the time, Pallas kernels for 0%

profile of v6, /device:TPU:2, one launch (start us, length us, event | category | flops | bytes accessed | tf_op | source)
XLA Modules:
  0.0 514.9 jit_solution(16297155270390426049)
XLA Ops:
  9.6 7.2 %collective-permute-start = (bf16[8,4120]{1,0:T(8,128)(2,1)S(1)}, bf16[8,4120]{1,0:T(8,128)(2,1)S(1)}, u32[]{:S(2)}, u32[]{:S(2)}) collective-permute-start(bf16[8,4120]{1,0:T(8,128)(2,1)S(1)} %concatenate.15), channel_id=1, source_target_pairs={{0,4},{1,5},{2,6},{3,7},{4,0},{5,1},{6,2},{7,3},{8,12},{9,13},{10,... | collective-permute-start | bytes 197768 | tf_op jit(solution)/shard_map/ppermute | solution.py:89
  22.5 7.2 %gather_fusion = bf16[256,4096]{1,0:T(8,128)(2,1)S(1)} fusion(bf16[2,8,4096]{2,1,0:T(8,128)(2,1)S(1)} %pad_maximum_fusion.1, s32[256]{0:T(256)S(1)} %fusion.24), kind=kCustom, calls=%fused_computation | custom fusion | bytes 4196352 | tf_op jit(solution)/shard_map/vmap(jit(_take))/gather | solution.py:100
  32.2 4.2 fusion.4
  37.6 55.8 %all_to_all.40 = bf16[32,8,4096]{2,1,0:T(8,128)(2,1)} all-to-all(bf16[32,8,4096]{2,1,0:T(8,128)(2,1)S(1)} %copy.51), channel_id=1, replica_groups=mesh['expert'=32,'replica'=8] {'expert'}, dimensions={0} | all-to-all | bytes 4194304 | tf_op jit(solution)/shard_map/all_to_all | solution.py:104
  93.5 86.5 %all-gather.5.cloned.1.call-done = bf16[128,8,4096]{2,1,0:T(8,128)(2,1)} async-done(((bf16[32,8,4096]{2,1,0:T(8,128)(2,1)}), bf16[128,8,4096]{2,1,0:T(8,128)(2,1)}) %all-gather.5.cloned.1.call-update) | async-done | bytes 8388624 | tf_op jit(solution)/shard_map/all_gather | solution.py:105
  180.0 6.8 %fusion.2 = f32[1024,192]{0,1:T(8,128)S(1)} fusion(bf16[128,8,4096]{2,1,0:T(8,128)(2,1)} %all-gather.5.cloned.1.call-done, bf16[1,192,4096]{2,1,0:T(8,128)(2,1)} %param.15), kind=kOutput, calls=%fused_computation.4 | convolution fusion | flops 1610612736 | bytes 10747904 | tf_op jit(solution)/shard_map/dot_general | solution.py:47
  186.8 4.4 fusion.13
  191.2 5.8 %collective-permute-start.1 = (bf16[1024,192]{0,1:T(8,128)(2,1)S(1)}, bf16[1024,192]{0,1:T(8,128)(2,1)S(1)}, u32[]{:S(2)}, u32[]{:S(2)}) collective-permute-start(bf16[1024,192]{0,1:T(8,128)(2,1)S(1)} %fusion.13), channel_id=1, source_target_pairs={{0,4},{1,5},{2,6},{3,7},{4,0},{5,1},{6,2},{7,3},{8,12},{9,13},{10,... | collective-permute-start | bytes 1179656 | tf_op jit(solution)/shard_map/ppermute | solution.py:109
  197.0 12.7 %collective-permute-done.1 = bf16[1024,192]{0,1:T(8,128)(2,1)S(1)} collective-permute-done((bf16[1024,192]{0,1:T(8,128)(2,1)S(1)}, bf16[1024,192]{0,1:T(8,128)(2,1)S(1)}, u32[]{:S(2)}, u32[]{:S(2)}) %collective-permute-start.1) | collective-permute-done | bytes 393248 | tf_op jit(solution)/shard_map/ppermute | solution.py:109
  213.8 13.9 %all-to-all-start.1 = ((bf16[192,8,512]{2,0,1:T(8,128)(2,1)}), bf16[192,8,512]{2,0,1:T(8,128)(2,1)S(1)}, u32[]{:S(2)}, u32[]{:S(2)}) async-start(bf16[192,8,512]{2,0,1:T(8,128)(2,1)} %copy.52), calls=%async_computation.1 | async-start | bytes 3145728 | tf_op jit(solution)/shard_map/all_to_all | solution.py:79
  231.3 37.8 %all-to-all-done.1 = bf16[192,8,512]{2,0,1:T(8,128)(2,1)S(1)} async-done(((bf16[192,8,512]{2,0,1:T(8,128)(2,1)}), bf16[192,8,512]{2,0,1:T(8,128)(2,1)S(1)}, u32[]{:S(2)}, u32[]{:S(2)}) %all-to-all-start.1) | async-done | bytes 1572896 | tf_op jit(solution)/shard_map/all_to_all | solution.py:79
  271.0 4.7 bitcast_convert_fusion
  275.7 3.6 all-to-all-start.2
  280.9 13.9 %all-to-all-done.2 = bf16[4,32,8,512]{3,2,1,0:T(8,128)(2,1)S(1)} async-done(((bf16[4,32,8,512]{3,2,1,0:T(8,128)(2,1)}), bf16[4,32,8,512]{3,2,1,0:T(8,128)(2,1)S(1)}, u32[]{:S(2)}, u32[]{:S(2)}) %all-to-all-start.2) | async-done | bytes 1048608 | tf_op jit(solution)/shard_map/all_to_all | solution.py:120
  299.3 7.2 %all-to-all-start.3 = ((bf16[32,8,2048]{2,1,0:T(8,128)(2,1)}), bf16[32,8,2048]{2,1,0:T(8,128)(2,1)S(1)}, u32[]{:S(2)}, u32[]{:S(2)}) async-start(bf16[32,8,2048]{2,1,0:T(8,128)(2,1)} %reshape.164), calls=%async_computation.3 | async-start | bytes 2097152 | tf_op jit(solution)/shard_map/all_to_all | solution.py:128
  306.5 100.7 %collective-permute-done.3 = bf16[1,192,4096]{2,1,0:T(8,128)(2,1)} collective-permute-done((bf16[1,192,4096]{2,1,0:T(8,128)(2,1)}, bf16[1,192,4096]{2,1,0:T(8,128)(2,1)}, u32[]{:S(2)}, u32[]{:S(2)}) %collective-permute-start.3) | collective-permute-done | bytes 1572896 | tf_op jit(solution)/shard_map/ppermute | solution.py:78
  407.2 2.7 broadcast_select_fusion.2
  409.9 31.0 %collective-permute-done.4 = bf16[1,192,4096]{2,1,0:T(8,128)(2,1)} collective-permute-done((bf16[1,192,4096]{2,1,0:T(8,128)(2,1)}, bf16[1,192,4096]{2,1,0:T(8,128)(2,1)}, u32[]{:S(2)}, u32[]{:S(2)}) %collective-permute-start.4) | collective-permute-done | bytes 1572896 | tf_op jit(solution)/shard_map/ppermute | solution.py:78
  440.9 2.7 broadcast_select_fusion.1
  443.6 31.0 %collective-permute-done.5 = bf16[1,192,4096]{2,1,0:T(8,128)(2,1)} collective-permute-done((bf16[1,192,4096]{2,1,0:T(8,128)(2,1)S(1)}, bf16[1,192,4096]{2,1,0:T(8,128)(2,1)}, u32[]{:S(2)}, u32[]{:S(2)}) %collective-permute-start.5) | collective-permute-done | bytes 1572896 | tf_op jit(solution)/shard_map/ppermute | solution.py:78
  475.9 9.7 %all-to-all-done.3 = bf16[32,8,2048]{2,1,0:T(8,128)(2,1)S(1)} async-done(((bf16[32,8,2048]{2,1,0:T(8,128)(2,1)}), bf16[32,8,2048]{2,1,0:T(8,128)(2,1)S(1)}, u32[]{:S(2)}, u32[]{:S(2)}) %all-to-all-start.3) | async-done | bytes 1048608 | tf_op jit(solution)/shard_map/all_to_all | solution.py:128
  490.9 5.7 %collective-permute-start.2 = (bf16[8,2048]{1,0:T(8,128)(2,1)S(1)}, bf16[8,2048]{1,0:T(8,128)(2,1)S(1)}, u32[]{:S(2)}, u32[]{:S(2)}) collective-permute-start(bf16[8,2048]{1,0:T(8,128)(2,1)S(1)} %get-tuple-element.23), channel_id=1, source_target_pairs={{0,4},{1,5},{2,6},{3,7},{4,0},{5,1},{6,2},{7,3},{8,12},{9,13},{10,... | collective-permute-start | bytes 98312 | tf_op jit(solution)/shard_map/ppermute | solution.py:139
  496.6 3.2 abs_reduce_fusion
  501.8 3.3 collective-permute-done.6
  (67 shorter events, 35.3 us)
Async XLA Ops:
  7.2 172.8 %all-gather.5.cloned.1.call-start = ((), (), s32[]{:S(2)}) async-start(), calls=%async_computation.4 | async-start | bytes 10485760 | tf_op jit(solution)/shard_map/all_gather | solution.py:105
  9.6 9.7 %collective-permute-start = (bf16[8,4120]{1,0:T(8,128)(2,1)S(1)}, bf16[8,4120]{1,0:T(8,128)(2,1)S(1)}, u32[]{:S(2)}, u32[]{:S(2)}) collective-permute-start(bf16[8,4120]{1,0:T(8,128)(2,1)S(1)} %concatenate.15), channel_id=1, source_target_pairs={{0,4},{1,5},{2,6},{3,7},{4,0},{5,1},{6,2},{7,3},{8,12},{9,13},{10,... | collective-permute-start | bytes 197768 | tf_op jit(solution)/shard_map/ppermute | solution.py:89
  93.4 177.5 %all-gather.7.cloned.1.call-start = ((), (), s32[]{:S(2)}) async-start(), calls=%async_computation.5 | async-start | bytes 3932160 | tf_op jit(solution)/shard_map/all_gather | solution.py:110
  180.0 6.9 %copy-start.3 = (bf16[128,8,4096]{2,1,0:T(8,128)(2,1)S(1)}, bf16[128,8,4096]{2,1,0:T(8,128)(2,1)}, u32[]{:S(2)}) copy-start(bf16[128,8,4096]{2,1,0:T(8,128)(2,1)} %all-gather.5.cloned.1.call-done) | copy-start | bytes 25165828
  191.2 18.5 %collective-permute-start.1 = (bf16[1024,192]{0,1:T(8,128)(2,1)S(1)}, bf16[1024,192]{0,1:T(8,128)(2,1)S(1)}, u32[]{:S(2)}, u32[]{:S(2)}) collective-permute-start(bf16[1024,192]{0,1:T(8,128)(2,1)S(1)} %fusion.13), channel_id=1, source_target_pairs={{0,4},{1,5},{2,6},{3,7},{4,0},{5,1},{6,2},{7,3},{8,12},{9,13},{10,... | collective-permute-start | bytes 1179656 | tf_op jit(solution)/shard_map/ppermute | solution.py:109
  209.8 1.7 copy-start
  213.8 17.4 %copy-start.2 = (s32[8,2]{0,1:T(2,128)S(1)}, s32[8,2]{0,1:T(2,128)}, u32[]{:S(2)}) copy-start(s32[8,2]{0,1:T(2,128)} %param.13) | copy-start | bytes 196
  213.8 55.3 %all-to-all-start.1 = ((bf16[192,8,512]{2,0,1:T(8,128)(2,1)}), bf16[192,8,512]{2,0,1:T(8,128)(2,1)S(1)}, u32[]{:S(2)}, u32[]{:S(2)}) async-start(bf16[192,8,512]{2,0,1:T(8,128)(2,1)} %copy.52), calls=%async_computation.1 | async-start | bytes 3145728 | tf_op jit(solution)/shard_map/all_to_all | solution.py:79
  227.7 179.4 %collective-permute-start.3 = (bf16[1,192,4096]{2,1,0:T(8,128)(2,1)}, bf16[1,192,4096]{2,1,0:T(8,128)(2,1)}, u32[]{:S(2)}, u32[]{:S(2)}) collective-permute-start(bf16[1,192,4096]{2,1,0:T(8,128)(2,1)} %param.15), channel_id=1, source_target_pairs={{0,128},{8,136},{16,144},{24,152},{32,160},{40,168},{48,176},{56,1... | collective-permute-start | bytes 4718600 | tf_op jit(solution)/shard_map/ppermute | solution.py:78
  228.2 212.6 %collective-permute-start.4 = (bf16[1,192,4096]{2,1,0:T(8,128)(2,1)}, bf16[1,192,4096]{2,1,0:T(8,128)(2,1)}, u32[]{:S(2)}, u32[]{:S(2)}) collective-permute-start(bf16[1,192,4096]{2,1,0:T(8,128)(2,1)} %param.16), channel_id=1, source_target_pairs={{0,128},{8,136},{16,144},{24,152},{32,160},{40,168},{48,176},{56,1... | collective-permute-start | bytes 4718600 | tf_op jit(solution)/shard_map/ppermute | solution.py:78
  230.7 243.9 %collective-permute-start.5 = (bf16[1,192,4096]{2,1,0:T(8,128)(2,1)S(1)}, bf16[1,192,4096]{2,1,0:T(8,128)(2,1)}, u32[]{:S(2)}, u32[]{:S(2)}) collective-permute-start(bf16[1,192,4096]{2,1,0:T(8,128)(2,1)S(1)} %copy-done), channel_id=1, source_target_pairs={{0,128},{8,136},{16,144},{24,152},{32,160},{40,168},{48,176},{56,1... | collective-permute-start | bytes 4718600 | tf_op jit(solution)/shard_map/ppermute | solution.py:78
  275.7 4.9 copy-start.1
  275.7 19.2 %all-to-all-start.2 = ((bf16[4,32,8,512]{3,2,1,0:T(8,128)(2,1)}), bf16[4,32,8,512]{3,2,1,0:T(8,128)(2,1)S(1)}, u32[]{:S(2)}, u32[]{:S(2)}) async-start(bf16[4,32,8,512]{3,2,1,0:T(8,128)(2,1)} %bitcast.90), calls=%async_computation.2 | async-start | bytes 2097152 | tf_op jit(solution)/shard_map/all_to_all | solution.py:120
  299.3 186.4 %all-to-all-start.3 = ((bf16[32,8,2048]{2,1,0:T(8,128)(2,1)}), bf16[32,8,2048]{2,1,0:T(8,128)(2,1)S(1)}, u32[]{:S(2)}, u32[]{:S(2)}) async-start(bf16[32,8,2048]{2,1,0:T(8,128)(2,1)} %reshape.164), calls=%async_computation.3 | async-start | bytes 2097152 | tf_op jit(solution)/shard_map/all_to_all | solution.py:128
  490.9 15.4 %collective-permute-start.2 = (bf16[8,2048]{1,0:T(8,128)(2,1)S(1)}, bf16[8,2048]{1,0:T(8,128)(2,1)S(1)}, u32[]{:S(2)}, u32[]{:S(2)}) collective-permute-start(bf16[8,2048]{1,0:T(8,128)(2,1)S(1)} %get-tuple-element.23), channel_id=1, source_target_pairs={{0,4},{1,5},{2,6},{3,7},{4,0},{5,1},{6,2},{7,3},{8,12},{9,13},{10,... | collective-permute-start | bytes 98312 | tf_op jit(solution)/shard_map/ppermute | solution.py:139
  500.4 4.7 collective-permute-start.6
Sparse Core Ops, SparseCore 0:
  93.6 86.3 all-gather.4
  210.9 60.0 all-gather.6

commit v7 on v3

--- a/solution.py
+++ b/solution.py
@@ -63,7 +63,6 @@
     replicas = lax.axis_size("replica")
     tok_rows, width = tokens.shape
     units = w_gate.shape[1]
-    cols = width // replicas
     ys = replicas // HALVES
     partner = pair_partner(swap_pairs, experts)
     me = lax.axis_index("expert")
@@ -77,12 +76,13 @@
     ygroups = [[h * ys + j for j in range(ys)] for h in range(HALVES)]
     arrived = tuple(lax.ppermute(w, "expert", ring) for w in (w_gate, w_up, w_down))
     down_cols = lax.all_to_all(
-        w_down[0].reshape(units, replicas, cols),
+        w_down[0].reshape(units, ys, width // ys),
         "replica",
         split_axis=1,
         concat_axis=0,
         tiled=True,
-    ).reshape(replicas, units, cols)
+        axis_index_groups=ygroups,
+    ).reshape(ys, units, width // ys)
     blk_tokens = canonical(tokens, lax.ppermute(tokens, "replica", across), first)
     blk_ids = canonical(expert_ids, lax.ppermute(expert_ids, "replica", across), first)
     blk_gw = canonical(gate_weights, lax.ppermute(gate_weights, "replica", across), first)
@@ -92,16 +92,15 @@
     picked = jax.vmap(lambda t, s: jnp.take(t, s, axis=0))(blk_tokens, source)
     outgoing = jnp.where(filled[..., None], picked, jnp.zeros((), jnp.bfloat16))
     outgoing = outgoing.reshape(HALVES, experts, CAP, width).transpose(1, 0, 2, 3)
+    outgoing = outgoing.reshape(experts, HALVES * CAP, width)
     arrived_rows = lax.all_to_all(outgoing, "expert", 0, 0, tiled=True)
     group_rows = lax.all_gather(
         arrived_rows, "replica", axis=0, tiled=False, axis_index_groups=ygroups
     )
     hidden = expert_hidden(group_rows, w_gate[0], w_up[0]).reshape(-1, units)
-    pair_hidden = canonical(hidden, lax.ppermute(hidden, "replica", across), first)
-    hidden_all = lax.all_gather(
-        pair_hidden, "replica", axis=1, tiled=False, axis_index_groups=ygroups
-    ).reshape(replicas, -1, units)
-    group_peak = jnp.max(jnp.abs(hidden_all)).astype(jnp.float32)
+    hidden_all = lax.all_gather(hidden, "replica", axis=0, tiled=False, axis_index_groups=ygroups)
+    half_peak = jnp.max(jnp.abs(hidden_all)).astype(jnp.float32)
+    group_peak = jnp.maximum(half_peak, lax.ppermute(half_peak, "replica", across))
     out_cols = lax.dot_general(
         hidden_all,
         down_cols,
@@ -109,30 +108,24 @@
         preferred_element_type=jnp.float32,
     ).astype(jnp.bfloat16)
     half_rows = lax.all_to_all(
-        out_cols.reshape(ys, experts, HALVES, CAP, cols),
+        out_cols.reshape(ys, experts, HALVES * CAP, width // ys),
         "replica",
         split_axis=0,
-        concat_axis=4,
+        concat_axis=3,
         tiled=True,
         axis_index_groups=ygroups,
     )
     returned = lax.all_to_all(
-        half_rows.reshape(experts, HALVES, CAP, ys * cols), "expert", 0, 0, tiled=True
-    )
-    by_block = returned.transpose(1, 0, 2, 3).reshape(HALVES, experts * CAP, ys * cols)
+        half_rows.reshape(experts, HALVES * CAP, width), "expert", 0, 0, tiled=True
+    ).reshape(experts, HALVES, CAP, width)
+    by_block = returned.transpose(1, 0, 2, 3).reshape(HALVES, experts * CAP, width)
     fetched = jax.vmap(lambda t, s: jnp.take(t, s, axis=0))(by_block, slot_of)
     scales = jnp.where(slot_kept, blk_gw.reshape(HALVES, -1), jnp.float32(0.0))
-    combined = jnp.sum(
-        (scales[..., None] * fetched).reshape(HALVES, tok_rows, TOPK, ys * cols), axis=2
-    )
+    combined = jnp.sum((scales[..., None] * fetched).reshape(HALVES, tok_rows, TOPK, width), axis=2)
     own_half = jnp.where(first, combined[0], combined[1])
     send_half = jnp.where(first, combined[1], combined[0])
     recv_half = lax.ppermute(send_half, "replica", across)
-    moe_output = jnp.where(
-        first,
-        jnp.concatenate([own_half, recv_half], axis=1),
-        jnp.concatenate([recv_half, own_half], axis=1),
-    ).astype(jnp.bfloat16)
+    moe_output = (own_half + recv_half).astype(jnp.bfloat16)
     moved_gate, moved_up, moved_down = (
         jnp.where(swapped, got, own) for got, own in zip(arrived, (w_gate, w_up, w_down))
     )

time: 524 us -> 540 us (1.031); the launches traced: 523 us -> 530 us
  blocking collectives: 54.6 us -> 89 us
  starting transfers between devices: 56.3 us -> 37.9 us
  local copies, waits for them, and re-layouts: 42.1 us -> 35.7 us
    all_to_all x0 -> x1, blocking collectives: none -> 34.4 us  [shards(): lax.all_to_all(w_down[0].reshape(units, ys, width // ys), 'replica', spli...]
    all_gather x1, waiting for transfers between devices: 33.4 us -> 2.62 us  [shards(): lax.all_gather(hidden, 'replica', axis=0, tiled=False, axis_index_groups=...]
    all_to_all x3 -> x2, waiting for transfers between devices: 8.33 us -> 33.4 us  [the longest x1 17.2 us: shards(): lax.all_to_all(out_cols.reshape(ys, experts, HALVES * CAP, width // ys),...]
    ppermute x3, waiting for transfers between devices: 94.4 us -> 116 us  [shards(): lax.ppermute(w, 'expert', ring)]
    all_to_all x3 -> x2, starting transfers between devices: 26.4 us -> 11.9 us  [the longest x1 8.15 us: shards(): lax.all_to_all(half_rows.reshape(experts, HALVES * CAP, width), 'expert',...]
    reshape x7 -> x3, local copies, waits for them, and re-layouts: 19.7 us -> 8.14 us  [the longest x1 4.45 us: shards(): half_rows.reshape(experts, HALVES * CAP, width)]
    ppermute x1, waiting for transfers between devices: 74 us -> 65.7 us  [shards(): lax.ppermute(gate_weights, 'replica', across)]
    ppermute x1, waiting for transfers between devices: 12.7 us -> 5.82 us  [shards(): lax.ppermute(half_peak, 'replica', across)]
  transfers between devices with their start and end apart: 14 -> 13, of which waited for: 10 -> 11; matrix products, arithmetic and copies ran while one was open for 7% -> 5% of each run, Pallas kernels for 0% -> 0%
where the time goes in v7:
time: 540 us; the launch traced here: 530 us
  waiting for transfers between devices  317 us (59%)
  blocking collectives  89 us (16%)
  starting transfers between devices  37.9 us (7%)
  local copies, waits for them, and re-layouts  35.7 us (7%)
  between operations  18.9 us (3%)
  other arithmetic  16.4 us (3%)
  matrix products  14.7 us (3%)
    ppermute x3, waiting for transfers between devices, shards(): lax.ppermute(w, 'expert', ring)  116 us
    all_gather x1, waiting for transfers between devices, shards(): lax.all_gather(arrived_rows, 'replica', axis=0, tiled=False, axis_index_g...  82.9 us
    ppermute x1, waiting for transfers between devices, shards(): lax.ppermute(gate_weights, 'replica', across)  65.7 us
    all_to_all x1, blocking collectives, shards(): arrived_rows = lax.all_to_all(outgoing, 'expert', 0, 0, tiled=True)  54.6 us
    all_to_all x1, blocking collectives, shards(): lax.all_to_all(w_down[0].reshape(units, ys, width // ys), 'replica', spli...  34.4 us
    all_to_all x1, waiting for transfers between devices, shards(): lax.all_to_all(out_cols.reshape(ys, experts, HALVES * CAP, width // ys),...  17.2 us
    all_to_all x1, waiting for transfers between devices, shards(): lax.all_to_all(half_rows.reshape(experts, HALVES * CAP, width), 'expert',...  16.2 us
  transfers between devices with their start and end apart: 13, of which 11 were waited for; matrix products, arithmetic and copies ran while one was open for 5% of the time, Pallas kernels for 0%

profile of v7, /device:TPU:2, one launch (start us, length us, event | category | flops | bytes accessed | tf_op | source)
XLA Modules:
  0.0 529.8 jit_solution(12691047088098454103)
XLA Ops:
  7.2 7.3 %collective-permute-start.2 = (bf16[8,4096]{1,0:T(8,128)(2,1)}, bf16[8,4096]{1,0:T(8,128)(2,1)S(1)}, u32[]{:S(2)}, u32[]{:S(2)}) collective-permute-start(bf16[8,4096]{1,0:T(8,128)(2,1)} %param.9), channel_id=1, source_target_pairs={{0,4},{1,5},{2,6},{3,7},{4,0},{5,1},{6,2},{7,3},{8,12},{9,13},{10,... | collective-permute-start | bytes 196616 | tf_op jit(solution)/shard_map/ppermute | solution.py:86
  14.6 7.7 %collective-permute-done = s32[8,8]{1,0:T(8,128)S(1)} collective-permute-done((s32[8,8]{1,0:T(8,128)}, s32[8,8]{1,0:T(8,128)S(1)}, u32[]{:S(2)}, u32[]{:S(2)}) %collective-permute-start) | collective-permute-done | bytes 288 | tf_op jit(solution)/shard_map/ppermute | solution.py:87
  25.8 7.2 %gather_fusion = bf16[256,4096]{1,0:T(8,128)(2,1)S(1)} fusion(bf16[2,8,4096]{2,1,0:T(8,128)(2,1)S(1)} %pad_maximum_fusion, s32[256]{0:T(256)S(1)} %fusion.26), kind=kCustom, calls=%fused_computation | custom fusion | bytes 4196352 | tf_op jit(solution)/shard_map/vmap(jit(_take))/gather | solution.py:92
  35.2 4.2 fusion.4
  40.6 54.6 %all_to_all.40 = bf16[32,8,4096]{2,1,0:T(8,128)(2,1)} all-to-all(bf16[32,8,4096]{2,1,0:T(8,128)(2,1)S(1)} %copy.53), channel_id=1, replica_groups=mesh['expert'=32,'replica'=8] {'expert'}, dimensions={0} | all-to-all | bytes 4194304 | tf_op jit(solution)/shard_map/all_to_all | solution.py:96
  95.2 82.9 %all-gather.5.cloned.1.call-done = bf16[128,8,4096]{2,1,0:T(8,128)(2,1)} async-done(((bf16[32,8,4096]{2,1,0:T(8,128)(2,1)}), bf16[128,8,4096]{2,1,0:T(8,128)(2,1)}) %all-gather.5.cloned.1.call-update) | async-done | bytes 8388624 | tf_op jit(solution)/shard_map/all_gather | solution.py:97
  178.2 6.4 %fusion.2 = f32[1024,192]{0,1:T(8,128)S(1)} fusion(bf16[128,8,4096]{2,1,0:T(8,128)(2,1)} %all-gather.5.cloned.1.call-done, bf16[1,192,4096]{2,1,0:T(8,128)(2,1)S(1)} %copy-done.4), kind=kOutput, calls=%fused_computation.4 | convolution fusion | flops 1610612736 | bytes 10747904 | tf_op jit(solution)/shard_map/dot_general | solution.py:47
  184.6 3.7 fusion.15
  190.0 34.4 %all_to_all.41 = bf16[192,4,1024]{2,0,1:T(8,128)(2,1)S(1)} all-to-all(bf16[192,4,1024]{2,0,1:T(8,128)(2,1)S(1)} %copy.54), channel_id=1, replica_groups={{0,1,2,3},{4,5,6,7},{8,9,10,11},{12,13,14,15},{16,17,18,19},{20,21,22,2..., dimensions={1} | all-to-all | bytes 3145728 | tf_op jit(solution)/shard_map/all_to_all | solution.py:78
  227.0 4.6 bitcast_convert_fusion
  231.6 3.7 all-to-all-start.2
  240.9 3.9 collective-permute-start.1
  244.9 17.2 %all-to-all-done.2 = bf16[4,32,8,1024]{3,2,1,0:T(8,128)(2,1)S(1)} async-done(((bf16[4,32,8,1024]{3,2,1,0:T(8,128)(2,1)}), bf16[4,32,8,1024]{3,2,1,0:T(8,128)(2,1)S(1)}, u32[]{:S(2)}, u32[]{:S(2)}) %all-to-all-start.2) | async-done | bytes 2097184 | tf_op jit(solution)/shard_map/all_to_all | solution.py:110
  265.4 4.5 reshape.168
  269.8 8.1 %all-to-all-start.3 = ((bf16[32,8,4096]{2,1,0:T(8,128)(2,1)}), bf16[32,8,4096]{2,1,0:T(8,128)(2,1)S(1)}, u32[]{:S(2)}, u32[]{:S(2)}) async-start(bf16[32,8,4096]{2,1,0:T(8,128)(2,1)} %reshape.168), calls=%async_computation.3 | async-start | bytes 4194304 | tf_op jit(solution)/shard_map/all_to_all | solution.py:118
  279.3 65.7 %collective-permute-done.1 = f32[8,8]{1,0:T(8,128)S(1)} collective-permute-done((f32[8,8]{1,0:T(8,128)S(1)}, f32[8,8]{1,0:T(8,128)S(1)}, u32[]{:S(2)}, u32[]{:S(2)}) %collective-permute-start.1) | collective-permute-done | bytes 288 | tf_op jit(solution)/shard_map/ppermute | solution.py:88
  345.3 52.4 %collective-permute-done.6 = bf16[1,192,4096]{2,1,0:T(8,128)(2,1)} collective-permute-done((bf16[1,192,4096]{2,1,0:T(8,128)(2,1)}, bf16[1,192,4096]{2,1,0:T(8,128)(2,1)}, u32[]{:S(2)}, u32[]{:S(2)}) %collective-permute-start.6) | collective-permute-done | bytes 1572896 | tf_op jit(solution)/shard_map/ppermute | solution.py:77
  400.4 31.0 %collective-permute-done.5 = bf16[1,192,4096]{2,1,0:T(8,128)(2,1)} collective-permute-done((bf16[1,192,4096]{2,1,0:T(8,128)(2,1)}, bf16[1,192,4096]{2,1,0:T(8,128)(2,1)}, u32[]{:S(2)}, u32[]{:S(2)}) %collective-permute-start.5) | collective-permute-done | bytes 1572896 | tf_op jit(solution)/shard_map/ppermute | solution.py:77
  432.8 32.4 %collective-permute-done.4 = bf16[1,192,4096]{2,1,0:T(8,128)(2,1)} collective-permute-done((bf16[1,192,4096]{2,1,0:T(8,128)(2,1)}, bf16[1,192,4096]{2,1,0:T(8,128)(2,1)}, u32[]{:S(2)}, u32[]{:S(2)}) %collective-permute-start.4) | collective-permute-done | bytes 1572896 | tf_op jit(solution)/shard_map/ppermute | solution.py:77
  466.5 3.8 reshape.185
  470.3 16.2 %all-to-all-done.3 = bf16[32,8,4096]{2,1,0:T(8,128)(2,1)S(1)} async-done(((bf16[32,8,4096]{2,1,0:T(8,128)(2,1)}), bf16[32,8,4096]{2,1,0:T(8,128)(2,1)S(1)}, u32[]{:S(2)}, u32[]{:S(2)}) %all-to-all-start.3) | async-done | bytes 2097184 | tf_op jit(solution)/shard_map/all_to_all | solution.py:118
  493.2 3.9 gather_fusion.1
  497.9 5.8 %collective-permute-start.3 = (f32[8,4096]{1,0:T(8,128)S(1)}, f32[8,4096]{1,0:T(8,128)S(1)}, u32[]{:S(2)}, u32[]{:S(2)}) collective-permute-start(f32[8,4096]{1,0:T(8,128)S(1)} %select_bitcast_fusion), channel_id=1, source_target_pairs={{0,4},{1,5},{2,6},{3,7},{4,0},{5,1},{6,2},{7,3},{8,12},{9,13},{10,... | collective-permute-start | bytes 393224 | tf_op jit(solution)/shard_map/ppermute | solution.py:127
  508.5 5.8 %collective-permute-done.7 = f32[]{:T(128)} collective-permute-done((f32[]{:T(128)}, f32[]{:T(128)}, u32[]{:S(2)}, u32[]{:S(2)}) %collective-permute-start.7) | collective-permute-done | bytes 36 | tf_op jit(solution)/shard_map/ppermute | solution.py:103
  (76 shorter events, 43.5 us)
Async XLA Ops:
  7.2 171.0 %all-gather.5.cloned.1.call-start = ((), (), s32[]{:S(2)}) async-start(), calls=%async_computation.4 | async-start | bytes 10485760 | tf_op jit(solution)/shard_map/all_gather | solution.py:97
  7.2 17.7 %collective-permute-start.2 = (bf16[8,4096]{1,0:T(8,128)(2,1)}, bf16[8,4096]{1,0:T(8,128)(2,1)S(1)}, u32[]{:S(2)}, u32[]{:S(2)}) collective-permute-start(bf16[8,4096]{1,0:T(8,128)(2,1)} %param.9), channel_id=1, source_target_pairs={{0,4},{1,5},{2,6},{3,7},{4,0},{5,1},{6,2},{7,3},{8,12},{9,13},{10,... | collective-permute-start | bytes 196616 | tf_op jit(solution)/shard_map/ppermute | solution.py:86
  14.5 7.8 %collective-permute-start = (s32[8,8]{1,0:T(8,128)}, s32[8,8]{1,0:T(8,128)S(1)}, u32[]{:S(2)}, u32[]{:S(2)}) collective-permute-start(s32[8,8]{1,0:T(8,128)} %param.10), channel_id=1, source_target_pairs={{0,4},{1,5},{2,6},{3,7},{4,0},{5,1},{6,2},{7,3},{8,12},{9,13},{10,... | collective-permute-start | bytes 776 | tf_op jit(solution)/shard_map/ppermute | solution.py:87
  95.1 83.0 %copy-start.4 = (bf16[1,192,4096]{2,1,0:T(8,128)(2,1)S(1)}, bf16[1,192,4096]{2,1,0:T(8,128)(2,1)}, u32[]{:S(2)}) copy-start(bf16[1,192,4096]{2,1,0:T(8,128)(2,1)} %param.15) | copy-start | bytes 4718596
  95.2 89.4 %copy-start.2 = (bf16[1,192,4096]{2,1,0:T(8,128)(2,1)S(1)}, bf16[1,192,4096]{2,1,0:T(8,128)(2,1)}, u32[]{:S(2)}) copy-start(bf16[1,192,4096]{2,1,0:T(8,128)(2,1)} %param.16) | copy-start | bytes 4718596
  95.2 131.8 %all-gather.7.cloned.1.call-start = ((), (), s32[]{:S(2)}) async-start(), calls=%async_computation.5 | async-start | bytes 1966080 | tf_op jit(solution)/shard_map/all_gather | solution.py:101
  178.2 6.4 %copy-start.8 = (bf16[128,8,4096]{2,1,0:T(8,128)(2,1)S(1)}, bf16[128,8,4096]{2,1,0:T(8,128)(2,1)}, u32[]{:S(2)}) copy-start(bf16[128,8,4096]{2,1,0:T(8,128)(2,1)} %all-gather.5.cloned.1.call-done) | copy-start | bytes 25165828
  184.6 3.7 copy-start
  231.6 9.3 %copy-start.6 = (f32[8,8]{1,0:T(8,128)S(1)}, f32[8,8]{1,0:T(8,128)}, u32[]{:S(2)}) copy-start(f32[8,8]{1,0:T(8,128)} %param.11) | copy-start | bytes 772
  231.6 13.3 %copy-start.7 = (s32[8,2]{0,1:T(2,128)S(1)}, s32[8,2]{0,1:T(2,128)}, u32[]{:S(2)}) copy-start(s32[8,2]{0,1:T(2,128)} %param.13) | copy-start | bytes 196
  231.6 30.5 %all-to-all-start.2 = ((bf16[4,32,8,1024]{3,2,1,0:T(8,128)(2,1)}), bf16[4,32,8,1024]{3,2,1,0:T(8,128)(2,1)S(1)}, u32[]{:S(2)}, u32[]{:S(2)}) async-start(bf16[4,32,8,1024]{3,2,1,0:T(8,128)(2,1)} %bitcast.84), calls=%async_computation.2 | async-start | bytes 4194304 | tf_op jit(solution)/shard_map/all_to_all | solution.py:110
  235.4 162.3 %collective-permute-start.6 = (bf16[1,192,4096]{2,1,0:T(8,128)(2,1)}, bf16[1,192,4096]{2,1,0:T(8,128)(2,1)}, u32[]{:S(2)}, u32[]{:S(2)}) collective-permute-start(bf16[1,192,4096]{2,1,0:T(8,128)(2,1)} %param.17), channel_id=1, source_target_pairs={{0,128},{8,136},{16,144},{24,152},{32,160},{40,168},{48,176},{56,1... | collective-permute-start | bytes 4718600 | tf_op jit(solution)/shard_map/ppermute | solution.py:77
  238.0 193.4 %collective-permute-start.5 = (bf16[1,192,4096]{2,1,0:T(8,128)(2,1)}, bf16[1,192,4096]{2,1,0:T(8,128)(2,1)}, u32[]{:S(2)}, u32[]{:S(2)}) collective-permute-start(bf16[1,192,4096]{2,1,0:T(8,128)(2,1)} %param.16), channel_id=1, source_target_pairs={{0,128},{8,136},{16,144},{24,152},{32,160},{40,168},{48,176},{56,1... | collective-permute-start | bytes 4718600 | tf_op jit(solution)/shard_map/ppermute | solution.py:77
  238.4 226.7 %collective-permute-start.4 = (bf16[1,192,4096]{2,1,0:T(8,128)(2,1)}, bf16[1,192,4096]{2,1,0:T(8,128)(2,1)}, u32[]{:S(2)}, u32[]{:S(2)}) collective-permute-start(bf16[1,192,4096]{2,1,0:T(8,128)(2,1)} %param.15), channel_id=1, source_target_pairs={{0,128},{8,136},{16,144},{24,152},{32,160},{40,168},{48,176},{56,1... | collective-permute-start | bytes 4718600 | tf_op jit(solution)/shard_map/ppermute | solution.py:77
  240.9 104.1 %collective-permute-start.1 = (f32[8,8]{1,0:T(8,128)S(1)}, f32[8,8]{1,0:T(8,128)S(1)}, u32[]{:S(2)}, u32[]{:S(2)}) collective-permute-start(f32[8,8]{1,0:T(8,128)S(1)} %copy-done.6), channel_id=1, source_target_pairs={{0,4},{1,5},{2,6},{3,7},{4,0},{5,1},{6,2},{7,3},{8,12},{9,13},{10,... | collective-permute-start | bytes 776 | tf_op jit(solution)/shard_map/ppermute | solution.py:88
  269.8 216.7 %all-to-all-start.3 = ((bf16[32,8,4096]{2,1,0:T(8,128)(2,1)}), bf16[32,8,4096]{2,1,0:T(8,128)(2,1)S(1)}, u32[]{:S(2)}, u32[]{:S(2)}) async-start(bf16[32,8,4096]{2,1,0:T(8,128)(2,1)} %reshape.168), calls=%async_computation.3 | async-start | bytes 4194304 | tf_op jit(solution)/shard_map/all_to_all | solution.py:118
  345.3 86.1 %copy-start.3 = (bf16[1,192,4096]{2,1,0:T(8,128)(2,1)S(1)}, bf16[1,192,4096]{2,1,0:T(8,128)(2,1)}, u32[]{:S(2)}) copy-start(bf16[1,192,4096]{2,1,0:T(8,128)(2,1)} %param.16) | copy-start | bytes 4718596
  400.4 64.7 %copy-start.5 = (bf16[1,192,4096]{2,1,0:T(8,128)(2,1)S(1)}, bf16[1,192,4096]{2,1,0:T(8,128)(2,1)}, u32[]{:S(2)}) copy-start(bf16[1,192,4096]{2,1,0:T(8,128)(2,1)} %param.15) | copy-start | bytes 4718596
  497.1 6.7 %copy-start.1 = (bf16[4,1024,192]{1,0,2:T(4,128)(2,1)S(1)}, bf16[4,1024,192]{1,0,2:T(4,128)(2,1)}, u32[]{:S(2)}) copy-start(bf16[4,1024,192]{1,0,2:T(4,128)(2,1)} %reshape.185) | copy-start | bytes 4718596
  497.9 22.8 %collective-permute-start.3 = (f32[8,4096]{1,0:T(8,128)S(1)}, f32[8,4096]{1,0:T(8,128)S(1)}, u32[]{:S(2)}, u32[]{:S(2)}) collective-permute-start(f32[8,4096]{1,0:T(8,128)S(1)} %select_bitcast_fusion), channel_id=1, source_target_pairs={{0,4},{1,5},{2,6},{3,7},{4,0},{5,1},{6,2},{7,3},{8,12},{9,13},{10,... | collective-permute-start | bytes 393224 | tf_op jit(solution)/shard_map/ppermute | solution.py:127
  506.6 7.7 %collective-permute-start.7 = (f32[]{:T(128)}, f32[]{:T(128)}, u32[]{:S(2)}, u32[]{:S(2)}) collective-permute-start(f32[]{:T(128)} %convert_element_type.24), channel_id=1, source_target_pairs={{0,4},{1,5},{2,6},{3,7},{4,0},{5,1},{6,2},{7,3},{8,12},{9,13},{10,... | collective-permute-start | bytes 20 | tf_op jit(solution)/shard_map/ppermute | solution.py:103
  515.5 4.7 collective-permute-start.8
Sparse Core Ops, SparseCore 0:
  95.3 82.8 all-gather.4
  188.5 38.5 all-gather.6
